TPU v7x, 512 devices: a whole 4x4x16 slice. The times are simulated.
512 devices in a mesh: req: 128 (over z, x, core), tp: 4 (over y).
Axes of the slice: x: 4, y: 4, z: 16, core: 2. Of those that a mesh axis runs over, the one named last changes fastest.
Arguments:
- queries: bfloat16 [16384, 3584], P('req', 'tp'), may hold values from -13 to 13
- tree_kv: bfloat16 [16384, 4, 256], P('req', 'tp'), may hold values from -5 to 5
- page_pool: bfloat16 [1536, 4, 128, 256], P('req', 'tp'), may hold values from -5 to 5
- page_table: int32 [256, 8], P('req'), may hold values from 0 to 11, as said below
- cache_len: int32 [256], P('req'), may hold values from 1 to 1024
- parents: int32 [256, 64], P('req'), may hold values from -1 to 62, as said below
- accepted: int32 [256], P('req'), may hold values from 0 to 63
- o_weight: bfloat16 [3584, 1792], P('tp'), may hold values from -0.5 to 0.5
Outputs:
- projected: bfloat16 [16384, 1792], P(('req', 'tp'))
- kept_rows: bfloat16 [16384, 4, 256], P('req', 'tp')
Inputs may be any that keep to these rules, and one draw needn't show every extreme that they name: Logical page k of request r is in slot page_table[r, k] of its own device's pool for k < 2, among that pool's first 4 slots, and for k >= 2 in that slot of the next req device's pool (the first device after the last), among its last 8 slots; distinct pages are in distinct slots; entries at k >= ceil(cache_len[r] / 128) are 0. parents[r, 0] = -1 and 0 <= parents[r, j] < j for j >= 1.
All inputs are finite; a program needn't handle non-finite values.
Results may differ from a plain program's by a relative error of at most 0.007.
Values may be sent and summed in bfloat16 or wider, within the bound.
No kernel may reach another device: no remote copies, remote signals or barrier semaphores. Data moves between devices by JAX's collectives and lax.ppermute only.
A program may use at most 64 MiB of HBM per device.

v0:
```python
import math

import jax
import jax.numpy as jnp
from jax import lax
from jax.sharding import PartitionSpec as P

HEAD_SIZE = 128
LOCAL = 2


very_negative = -1e30


def from_behind(block, axis, distance):
    devices = range(lax.axis_size(axis))
    route = [((i - distance) % len(devices), i) for i in devices]
    return lax.ppermute(block, axis, route)


def ancestors(parent_row):
    tree_len = parent_row.shape[0]
    node_ids = jnp.arange(tree_len, dtype=jnp.int32)
    parent_links = (parent_row[:, None] == node_ids[None, :]).astype(jnp.float32)
    reachable = jnp.eye(tree_len, dtype=jnp.float32) + parent_links
    for squaring in range((tree_len - 1).bit_length()):
        reachable = jnp.minimum(jnp.dot(reachable, reachable, precision=lax.Precision.HIGHEST), 1.0)
    return reachable


def block_stats(query_rows, block_keys, block_values, visible):
    scores = jnp.einsum(
        "tgd,nd->tgn", query_rows, block_keys, preferred_element_type=jnp.float32
    ) * (1.0 / math.sqrt(query_rows.shape[-1]))
    scores = jnp.where(visible, scores, very_negative)
    maxima = jnp.max(scores, axis=-1)
    weights = jnp.where(visible, jnp.exp(scores - maxima[..., None]), 0.0).astype(jnp.bfloat16)
    totals = jnp.sum(weights.astype(jnp.float32), axis=-1)
    accums = jnp.einsum("tgn,nd->tgd", weights, block_values, preferred_element_type=jnp.float32)
    return (maxima, totals, accums)


def combine(first_state, second_state):
    joined_max = jnp.maximum(first_state[0], second_state[0])
    first_factor = jnp.exp(first_state[0] - joined_max)
    second_factor = jnp.exp(second_state[0] - joined_max)
    totals = first_factor * first_state[1] + second_factor * second_state[1]
    accums = first_factor[..., None] * first_state[2] + second_factor[..., None] * second_state[2]
    return (joined_max, totals, accums)


def pages_partial(query_rows, pages, visible):
    head_dim = query_rows.shape[-1]
    scores = jnp.einsum(
        "tgd,knd->tgkn", query_rows, pages[..., :head_dim], preferred_element_type=jnp.float32
    ) * (1.0 / math.sqrt(head_dim))
    mask = visible[None, None, :, :]
    scores = jnp.where(mask, scores, very_negative)
    maxima = jnp.max(scores, axis=-1)
    weights = jnp.where(mask, jnp.exp(scores - maxima[..., None]), 0.0).astype(jnp.bfloat16)
    totals = jnp.sum(weights.astype(jnp.float32), axis=-1)
    accums = jnp.einsum(
        "tgkn,knd->tgkd", weights, pages[..., head_dim:], preferred_element_type=jnp.float32
    )
    overall = jnp.max(maxima, axis=-1)
    factors = jnp.exp(maxima - overall[..., None])
    total = jnp.sum(factors * totals, axis=-1)
    accum = jnp.sum(factors[..., None] * accums, axis=2)
    return (overall, total, accum)


def sweep_all(query_rows, pool_slots, tables, lengths, first_page):
    page_len = pool_slots.shape[1]
    page_count = tables.shape[1]
    offsets = jnp.arange(page_len, dtype=jnp.int32)
    page_numbers = first_page + jnp.arange(page_count, dtype=jnp.int32)
    positions = page_numbers[:, None] * page_len + offsets[None, :]

    def one_request(request_data):
        request_query, table_row, length = request_data
        pages = jnp.take(pool_slots, table_row, axis=0)
        visible = positions < length
        return pages_partial(request_query, pages, visible)

    return lax.map(one_request, (query_rows, tables, lengths))


def shards(queries, tree_kv, page_pool, page_table, cache_len, parents, accepted, o_weight):
    requests = page_table.shape[0]
    tree_len = parents.shape[1]
    group_size = queries.shape[1] // HEAD_SIZE
    query_rows = queries.reshape(requests, tree_len, group_size, HEAD_SIZE)
    tree_rows = tree_kv[:, 0, :].reshape(requests, tree_len, 2 * HEAD_SIZE)
    pool_slots = page_pool[:, 0]
    reachable = jax.vmap(ancestors)(parents)
    page_meta = jnp.concatenate([page_table, cache_len[:, None]], axis=1)
    moved_queries, moved_meta = from_behind((queries, page_meta), "req", 1)
    moved_rows = moved_queries.reshape(requests, tree_len, group_size, HEAD_SIZE)
    partial_value = sweep_all(
        moved_rows, pool_slots, moved_meta[:, LOCAL:-1], moved_meta[:, -1], LOCAL
    )
    returned = from_behind((partial_value[2], partial_value[0], partial_value[1]), "req", -1)
    local_state = sweep_all(query_rows, pool_slots, page_table[:, :LOCAL], cache_len, 0)
    page_state = combine(local_state, (returned[1], returned[2], returned[0]))
    tree_visible = (reachable > 0.5)[:, :, None, :]
    tree_state = jax.vmap(block_stats)(
        query_rows, tree_rows[:, :, :HEAD_SIZE], tree_rows[:, :, HEAD_SIZE:], tree_visible
    )
    merged = combine(page_state, tree_state)
    attention = (
        (merged[2] / merged[1][..., None])
        .astype(jnp.bfloat16)
        .reshape(requests * tree_len, group_size * HEAD_SIZE)
    )
    rows_out = attention.shape[0] // lax.axis_size("tp")
    whole_sum = lax.psum(jnp.dot(attention, o_weight, preferred_element_type=jnp.float32), "tp")
    summed = lax.dynamic_slice_in_dim(whole_sum, lax.axis_index("tp") * rows_out, rows_out, 0)
    projected = summed.astype(jnp.bfloat16)
    node_ids = jnp.arange(tree_len, dtype=jnp.int32)
    leaf_onehot = (accepted[:, None] == node_ids[None, :]).astype(jnp.float32)
    kept_mask = jnp.einsum("rm,rmn->rn", leaf_onehot, reachable, precision=lax.Precision.HIGHEST)
    depths = jnp.sum(reachable, axis=2) - 1.0
    slot_ids = jnp.arange(tree_len, dtype=jnp.float32)
    selector = (
        kept_mask[:, None, :] * (depths[:, None, :] == slot_ids[None, :, None]).astype(jnp.float32)
    ).astype(jnp.bfloat16)
    kept = jnp.einsum(
        "rsm,rmc->rsc", selector, tree_rows, preferred_element_type=jnp.float32
    ).astype(jnp.bfloat16)
    return (projected, kept.reshape(requests * tree_len, 1, 2 * HEAD_SIZE))


def solution(mesh):
    in_specs = (
        P("req", "tp"),
        P("req", "tp", None),
        P("req", "tp", None, None),
        P("req", None),
        P("req"),
        P("req", None),
        P("req"),
        P("tp", None),
    )
    out_specs = (P(("req", "tp"), None), P("req", "tp", None))
    return jax.shard_map(shards, mesh=mesh, in_specs=in_specs, out_specs=out_specs, check_vma=False)
```

profile of v0, /device:TPU:8, one launch (start us, length us, event | category | flops | bytes accessed | tf_op | source)
XLA Modules:
  0.0 122.9 jit_solution(13484984771491410831)
XLA Ops:
  0.6 0.9 copy.48
  1.5 1.4 %pad_add_fusion = s32[2,9]{1,0:T(2,128)} fusion(s32[2,1]{1,0:T(2,128)S(1)} %copy.48, s32[2,8]{1,0:T(2,128)} %param.15), kind=kLoop, calls=%fused_computation.98 | loop fusion | flops 18 | bytes 144 | tf_op jit(solution)/shard_map/concatenate | solution.py:96
  2.9 1.9 %collective-permute-start = (s32[2,9]{1,0:T(2,128)}, s32[2,9]{1,0:T(2,128)}, u32[]{:S(2)}, u32[]{:S(2)}) collective-permute-start(s32[2,9]{1,0:T(2,128)} %pad_add_fusion), channel_id=1, source_target_pairs={{508,0},{0,4},{4,8},{8,12},{12,16},{16,20},{20,24},{24,28},{28,32}... | collective-permute-start | bytes 224 | tf_op jit(solution)/shard_map/ppermute | solution.py:18
  4.8 3.5 %collective-permute-start.1 = (bf16[128,896]{1,0:T(8,128)(2,1)}, bf16[128,896]{1,0:T(8,128)(2,1)}, u32[]{:S(2)}, u32[]{:S(2)}) collective-permute-start(bf16[128,896]{1,0:T(8,128)(2,1)} %param.12), channel_id=1, source_target_pairs={{508,0},{0,4},{4,8},{8,12},{12,16},{16,20},{20,24},{24,28},{28,32}... | collective-permute-start | bytes 688136 | tf_op jit(solution)/shard_map/ppermute | solution.py:18
  8.9 1.2 reshape.134
  10.1 1.3 %compare_bitcast_fusion = pred[2,64,1]{1,0,2:T(4,128)(4,1)} fusion(s32[2]{0:T(128)} %param.18), kind=kLoop, calls=%fused_computation.97 | loop fusion | flops 128 | bytes 136 | tf_op jit(solution)/shard_map/eq | solution.py:120
  11.4 1.0 convolution_minimum_fusion.5
  13.3 0.8 broadcast_compare_fusion
  14.1 0.8 copy.52
  14.9 0.7 reduce_sum.73
  15.6 1.4 %fusion.35 = f32[2,1,64]{2,1,0:T(1,128)} fusion(f32[2,64,64]{2,1,0:T(8,128)S(1)} %get-tuple-element.262, pred[2,64,1]{1,0,2:T(4,128)(4,1)} %compare_bitcast_fusion), kind=kOutput, calls=%fused_computation.95 | convolution fusion | flops 98304 | bytes 33408 | tf_op jit(solution)/shard_map/rm,rmn->rn/dot_general | solution.py:121
  17.0 0.7 copy.47
  17.7 0.8 broadcast.143.clone.1
  18.5 17.2 %while.30 = (s32[]{:T(128)}, f32[2,64,7]{1,2,0:T(8,128)S(1)}, f32[2,64,7]{1,2,0:T(8,128)S(1)}, f32[2,64,7,128]{3,1,2,0:T(8,128)}, s32[2]{0:T(128)}, /*index=5*/b...) while((s32[]{:T(128)}, f32[2,64,7]{1,2,0:T(8,128)S(1)}, ...), condition=%wide.region_6.7_spmd.clone, body=%wide.region_0.6_spmd.clone.sunk | while | flops 59991572 | bytes 6568445 | solution.py:85
  18.5 1.3 %dynamic_slice.66 = s32[1]{0:T(128)} dynamic-slice(s32[2]{0:T(128)} %get-tuple-element.465, s32[]{:T(128)S(6)} %copy.108), dynamic_slice_sizes={1} | dynamic-slice | bytes 12 | tf_op jit(solution)/shard_map/while/body/jit(dynamic_index_in_dim)/dynamic_slice | solution.py:85
  19.8 1.3 %add_compare_fusion.4 = pred[2,128]{1,0:T(4,128)(4,1)S(1)} fusion(s32[2]{0:T(128)} %get-tuple-element.469, s32[]{:T(128)} %bitcast.143), kind=kLoop, calls=%fused_computation.28.clone.1 | loop fusion | flops 512 | bytes 268 | tf_op jit(solution)/shard_map/while/body/eval_jaxpr/lt | solution.py:82
  21.1 0.7 fusion.67
  21.8 0.7 compare_and_fusion.4
  22.5 1.7 %gather_fusion = bf16[2,128,256]{2,1,0:T(8,128)(2,1)S(1)} fusion(bf16[12,128,256]{2,1,0:T(8,128)(2,1)} %get-tuple-element.468, s32[1024]{0:T(1024)S(1)} %pad_clamp_fusion.4), kind=kCustom, calls=%fused_computation.clone.clone.1 | custom fusion | bytes 262152 | tf_op jit(solution)/shard_map/while/body/eval_jaxpr/jit(_take)/gather | solution.py:81
  24.3 1.4 %fusion.68 = (f32[64,7,2]{0,2,1:T(2,128)S(1)}, f32[64,7]{0,1:T(8,128)S(1)}, f32[64,7,2,128]{3,0,2,1:T(8,128)S(1)}) fusion(bf16[2,128,256]{2,1,0:T(8,128)(2,1)S(1)} %broadcast_select_fusion.4, bf16[2,64,7,128]{3,1,2,0:T(8,128)(2,1)} %get-tuple-element.466, s32[]{:T(128)S(6)} %copy.108, pred[2,128]{1,0:T(4,128)(4,1)S(1)} %add_compare_fusion.4), kind=kOutput, calls=%fused_computation.105.clone.1 | convolution fusion | flops 29817536 | bytes 644868 | tf_op jit(solution)/shard_map/while/body/eval_jaxpr/tgd,knd->tgkn/dot_general | solution.py:54
  26.4 0.8 copy-done.3
  27.1 1.2 %dynamic_slice.66 = s32[1]{0:T(128)} dynamic-slice(s32[2]{0:T(128)} %get-tuple-element.465, s32[]{:T(128)S(6)} %copy.108), dynamic_slice_sizes={1} | dynamic-slice | bytes 12 | tf_op jit(solution)/shard_map/while/body/jit(dynamic_index_in_dim)/dynamic_slice | solution.py:85
  28.4 1.3 %add_compare_fusion.4 = pred[2,128]{1,0:T(4,128)(4,1)S(1)} fusion(s32[2]{0:T(128)} %get-tuple-element.469, s32[]{:T(128)} %bitcast.143), kind=kLoop, calls=%fused_computation.28.clone.1 | loop fusion | flops 512 | bytes 268 | tf_op jit(solution)/shard_map/while/body/eval_jaxpr/lt | solution.py:82
  29.7 0.7 fusion.67
  30.4 0.7 compare_and_fusion.4
  31.1 1.7 %gather_fusion = bf16[2,128,256]{2,1,0:T(8,128)(2,1)S(1)} fusion(bf16[12,128,256]{2,1,0:T(8,128)(2,1)} %get-tuple-element.468, s32[1024]{0:T(1024)S(1)} %pad_clamp_fusion.4), kind=kCustom, calls=%fused_computation.clone.clone.1 | custom fusion | bytes 262152 | tf_op jit(solution)/shard_map/while/body/eval_jaxpr/jit(_take)/gather | solution.py:81
  32.9 1.4 %fusion.68 = (f32[64,7,2]{0,2,1:T(2,128)S(1)}, f32[64,7]{0,1:T(8,128)S(1)}, f32[64,7,2,128]{3,0,2,1:T(8,128)S(1)}) fusion(bf16[2,128,256]{2,1,0:T(8,128)(2,1)S(1)} %broadcast_select_fusion.4, bf16[2,64,7,128]{3,1,2,0:T(8,128)(2,1)} %get-tuple-element.466, s32[]{:T(128)S(6)} %copy.108, pred[2,128]{1,0:T(4,128)(4,1)S(1)} %add_compare_fusion.4), kind=kOutput, calls=%fused_computation.105.clone.1 | convolution fusion | flops 29817536 | bytes 644868 | tf_op jit(solution)/shard_map/while/body/eval_jaxpr/tgd,knd->tgkn/dot_general | solution.py:54
  34.9 0.8 copy-done.3
  35.7 1.3 %fusion.43 = (f32[2,64,7]{1,2,0:T(8,128)S(1)}, f32[2,64,7,64]{1,3,2,0:T(8,128)S(1)}) fusion(bf16[2,64,7,128]{3,1,2,0:T(8,128)(2,1)} %get-tuple-element.472, bf16[2,64,256]{2,1,0:T(8,128)(2,1)S(1)} %bitcast.156, pred[2,64,64]{1,2,0:T(8,128)(4,1)S(1)} %copy.52), kind=kOutput, calls=%fused_computation.107 | convolution fusion | flops 14851200 | bytes 511488 | tf_op jit(solution)/shard_map/vmap(tgd,nd->tgn)/dot_general | solution.py:32
  37.0 0.8 copy-done.1
  37.8 1.0 fusion.26
  40.0 1.3 %slice.29 = s32[2,6]{1,0:T(2,128)} slice(s32[2,9]{1,0:T(2,128)} %collective-permute-done), slice={[0:2], [2:8]} | slice | bytes 96 | tf_op jit(solution)/shard_map/slice | solution.py:100
  41.3 1.4 %slice_reduce_fusion = s32[2]{0:T(128)} fusion(s32[2,9]{1,0:T(2,128)} %collective-permute-done), kind=kLoop, calls=%fused_computation.99 | loop fusion | bytes 16 | tf_op jit(solution)/shard_map/slice | solution.py:100
  42.7 1.2 reshape.135
  43.9 0.7 copy.49
  45.8 0.8 broadcast.143.clone
  46.7 23.4 %while.31 = (s32[]{:T(128)}, f32[2,64,7]{1,2,0:T(8,128)}, f32[2,64,7]{1,2,0:T(8,128)}, f32[2,64,7,128]{3,1,2,0:T(8,128)}, s32[2]{0:T(128)}, /*index=5*/bf16[2,64...) while((s32[]{:T(128)}, f32[2,64,7]{1,2,0:T(8,128)}, ...), condition=%wide.region_13.14_spmd.clone, body=%wide.region_7.13_spmd.clone.sunk | while | flops 180089152 | bytes 11682033 | solution.py:85
  46.7 1.3 %dynamic_slice.70 = s32[1]{0:T(128)} dynamic-slice(s32[2]{0:T(128)} %get-tuple-element.435, s32[]{:T(128)S(6)} %copy.96), dynamic_slice_sizes={1} | dynamic-slice | bytes 12 | tf_op jit(solution)/shard_map/while/body/jit(dynamic_index_in_dim)/dynamic_slice | solution.py:85
  48.0 1.4 %add_compare_fusion.5 = pred[6,128]{1,0:T(8,128)(4,1)S(1)} fusion(s32[6]{0:T(128)} %get-tuple-element.439, s32[]{:T(128)} %bitcast.153), kind=kLoop, calls=%fused_computation.49.clone.1 | loop fusion | flops 1536 | bytes 796 | tf_op jit(solution)/shard_map/while/body/eval_jaxpr/lt | solution.py:82
  49.4 0.7 fusion.71
  50.1 1.3 %compare_and_fusion.5 = pred[6]{0:T(512)(128)(4,1)} fusion(s32[2,6]{1,0:T(2,128)} %get-tuple-element.437, s32[]{:T(128)S(6)} %copy.96), kind=kLoop, calls=%fused_computation.52.clone.1 | loop fusion | flops 36 | bytes 34 | tf_op jit(solution)/shard_map/while/body/eval_jaxpr/jit(_take)/and | solution.py:81
  51.4 2.5 %gather_fusion.1 = bf16[6,128,256]{2,1,0:T(8,128)(2,1)} fusion(bf16[12,128,256]{2,1,0:T(8,128)(2,1)} %get-tuple-element.438, s32[1024]{0:T(1024)S(1)} %pad_clamp_fusion.5), kind=kCustom, calls=%fused_computation.1.clone.clone.1 | custom fusion | bytes 786456 | tf_op jit(solution)/shard_map/while/body/eval_jaxpr/jit(_take)/gather | solution.py:81
  53.9 1.1 broadcast_select_fusion.5
  55.0 0.7 fusion.72
  55.7 0.8 convert_reduce_fusion.6
  57.6 0.8 copy-done.5
  58.4 1.3 %dynamic_slice.70 = s32[1]{0:T(128)} dynamic-slice(s32[2]{0:T(128)} %get-tuple-element.435, s32[]{:T(128)S(6)} %copy.96), dynamic_slice_sizes={1} | dynamic-slice | bytes 12 | tf_op jit(solution)/shard_map/while/body/jit(dynamic_index_in_dim)/dynamic_slice | solution.py:85
  59.7 1.4 %add_compare_fusion.5 = pred[6,128]{1,0:T(8,128)(4,1)S(1)} fusion(s32[6]{0:T(128)} %get-tuple-element.439, s32[]{:T(128)} %bitcast.153), kind=kLoop, calls=%fused_computation.49.clone.1 | loop fusion | flops 1536 | bytes 796 | tf_op jit(solution)/shard_map/while/body/eval_jaxpr/lt | solution.py:82
  61.1 0.7 fusion.71
  61.8 1.3 %compare_and_fusion.5 = pred[6]{0:T(512)(128)(4,1)} fusion(s32[2,6]{1,0:T(2,128)} %get-tuple-element.437, s32[]{:T(128)S(6)} %copy.96), kind=kLoop, calls=%fused_computation.52.clone.1 | loop fusion | flops 36 | bytes 34 | tf_op jit(solution)/shard_map/while/body/eval_jaxpr/jit(_take)/and | solution.py:81
  63.1 2.5 %gather_fusion.1 = bf16[6,128,256]{2,1,0:T(8,128)(2,1)} fusion(bf16[12,128,256]{2,1,0:T(8,128)(2,1)} %get-tuple-element.438, s32[1024]{0:T(1024)S(1)} %pad_clamp_fusion.5), kind=kCustom, calls=%fused_computation.1.clone.clone.1 | custom fusion | bytes 786456 | tf_op jit(solution)/shard_map/while/body/eval_jaxpr/jit(_take)/gather | solution.py:81
  65.5 1.1 broadcast_select_fusion.5
  66.6 0.7 fusion.72
  67.4 0.8 convert_reduce_fusion.6
  69.3 0.8 copy-done.5
  70.0 11.4 %collective-permute-start.3 = (f32[2,64,7,128]{3,1,2,0:T(8,128)}, f32[2,64,7,128]{3,1,2,0:T(8,128)}, u32[]{:S(2)}, u32[]{:S(2)}) collective-permute-start(f32[2,64,7,128]{3,1,2,0:T(8,128)} %get-tuple-element.103), channel_id=1, source_target_pairs={{4,0},{8,4},{12,8},{16,12},{20,16},{24,20},{28,24},{32,28},{36,32}... | collective-permute-start | bytes 1376264 | tf_op jit(solution)/shard_map/ppermute | solution.py:18
  81.5 1.4 %convolution_convert_fusion = bf16[2,64,256]{2,1,0:T(8,128)(2,1)} fusion(bf16[2,64,256]{2,1,0:T(8,128)(2,1)S(1)} %bitcast.158, f32[2,64]{1,0:T(2,128)} %bitcast.160, f32[2,64]{1,0:T(2,128)} %broadcast_add_fusion), kind=kOutput, calls=%fused_computation.58 | convolution fusion | flops 4243456 | bytes 132096 | tf_op jit(solution)/shard_map/rsm,rmc->rsc/dot_general | solution.py:127
  82.9 2.6 %collective-permute-start.2 = (f32[2,64,7]{1,2,0:T(8,128)}, f32[2,64,7]{1,2,0:T(8,128)S(1)}, u32[]{:S(2)}, u32[]{:S(2)}) collective-permute-start(f32[2,64,7]{1,2,0:T(8,128)} %get-tuple-element.101), channel_id=1, source_target_pairs={{4,0},{8,4},{12,8},{16,12},{20,16},{24,20},{28,24},{32,28},{36,32}... | collective-permute-start | bytes 10760 | tf_op jit(solution)/shard_map/ppermute | solution.py:18
  85.5 3.7 %collective-permute-start.4 = (f32[2,64,7]{1,2,0:T(8,128)}, f32[2,64,7]{1,2,0:T(8,128)S(1)}, u32[]{:S(2)}, u32[]{:S(2)}) collective-permute-start(f32[2,64,7]{1,2,0:T(8,128)} %get-tuple-element.105), channel_id=1, source_target_pairs={{4,0},{8,4},{12,8},{16,12},{20,16},{24,20},{28,24},{32,28},{36,32}... | collective-permute-start | bytes 10760 | tf_op jit(solution)/shard_map/ppermute | solution.py:18
  89.2 1.1 convert_reduce_fusion.2
  90.8 1.9 %divide_convert_fusion = bf16[2,64,7,128]{3,1,2,0:T(8,128)(2,1)S(1)} fusion(f32[2,64,7,128]{3,1,2,0:T(8,128)} %fusion.26, f32[2,64,7,128]{3,1,2,0:T(8,128)} %collective-permute-done.3, f32[2,64,7,128]{3,1,2,0:T(8,128)} %get-tuple-element.102, f32[2,64,7]{1,2,0:T(8,128)S(1)} %get-tuple-element.250, f32[2,64,7]{1,2,0:T(8,128)S(1)} %get-tuple-element.254, ...), kind=kLoop, calls=%fused_computation.65 | loop fusion | flops 917504 | bytes 1623552 | tf_op jit(solution)/shard_map/convert_element_type | solution.py:112
  92.9 1.6 %fusion.21 = f32[128,1792]{1,0:T(8,128)} fusion(bf16[896,1792]{1,0:T(8,128)(2,1)S(1)} %copy-done, bf16[16,8,7,128]{3,2,1,0:T(8,128)(2,1)S(1)} %bitcast.155), kind=kOutput, calls=%fused_computation.68 | convolution fusion | flops 411041792 | bytes 4358144 | tf_op jit(solution)/shard_map/dot_general | solution.py:116
  94.5 26.9 %all-reduce.1 = bf16[128,1792]{1,0:T(8,128)(2,1)} all-reduce(f32[128,1792]{1,0:T(8,128)} %fusion.21), channel_id=1, replica_groups=mesh['req'=128,'tp'=4] {'tp'}, use_global_device_ids=true, to_apply=%region_16.17 | all-reduce | flops 229376 | bytes 1376256 | tf_op jit(solution)/shard_map/psum | solution.py:116
  121.4 1.6 %dynamic-slice_convert_fusion = bf16[32,1792]{1,0:T(8,128)(2,1)} fusion(bf16[128,1792]{1,0:T(8,128)(2,1)} %all-reduce.1, s32[]{:T(128)S(6)} %select_n.66), kind=kLoop, calls=%fused_computation.71 | loop fusion | bytes 229380 | tf_op jit(solution)/shard_map/convert_element_type | solution.py:118
  (98 shorter events, 7.8 us)
Async XLA Ops:
  0.6 92.2 %copy-start = (bf16[896,1792]{1,0:T(8,128)(2,1)S(1)}, bf16[896,1792]{1,0:T(8,128)(2,1)}, u32[]{:S(2)}) copy-start(bf16[896,1792]{1,0:T(8,128)(2,1)} %param.19) | copy-start | bytes 9633796
  2.9 37.1 %collective-permute-start = (s32[2,9]{1,0:T(2,128)}, s32[2,9]{1,0:T(2,128)}, u32[]{:S(2)}, u32[]{:S(2)}) collective-permute-start(s32[2,9]{1,0:T(2,128)} %pad_add_fusion), channel_id=1, source_target_pairs={{508,0},{0,4},{4,8},{8,12},{12,16},{16,20},{20,24},{24,28},{28,32}... | collective-permute-start | bytes 224 | tf_op jit(solution)/shard_map/ppermute | solution.py:18
  4.8 37.8 %collective-permute-start.1 = (bf16[128,896]{1,0:T(8,128)(2,1)}, bf16[128,896]{1,0:T(8,128)(2,1)}, u32[]{:S(2)}, u32[]{:S(2)}) collective-permute-start(bf16[128,896]{1,0:T(8,128)(2,1)} %param.12), channel_id=1, source_target_pairs={{508,0},{0,4},{4,8},{8,12},{12,16},{16,20},{20,24},{24,28},{28,32}... | collective-permute-start | bytes 688136 | tf_op jit(solution)/shard_map/ppermute | solution.py:18
  18.5 17.2 %copy-start.6 = (bf16[128,1,256]{2,0,1:T(8,128)(2,1)S(1)}, bf16[128,1,256]{2,0,1:T(8,128)(2,1)}, u32[]{:S(2)}) copy-start(bf16[128,1,256]{2,0,1:T(8,128)(2,1)} %param.13) | copy-start | bytes 196612
  24.2 2.1 %copy-start.2 = (f32[2,64,7,128]{3,1,2,0:T(8,128)S(1)}, f32[2,64,7,128]{3,1,2,0:T(8,128)}, u32[]{:S(2)}) copy-start(f32[2,64,7,128]{3,1,2,0:T(8,128)} %get-tuple-element.454) | copy-start | bytes 1376260 | tf_op jit(solution)/shard_map/while
  26.4 0.8 copy-start.3
  32.8 2.1 %copy-start.2 = (f32[2,64,7,128]{3,1,2,0:T(8,128)S(1)}, f32[2,64,7,128]{3,1,2,0:T(8,128)}, u32[]{:S(2)}) copy-start(f32[2,64,7,128]{3,1,2,0:T(8,128)} %get-tuple-element.454) | copy-start | bytes 1376260 | tf_op jit(solution)/shard_map/while
  34.9 0.8 copy-start.3
  35.7 7.0 %copy-start.10 = (f32[2,64,7]{1,2,0:T(8,128)}, f32[2,64,7]{1,2,0:T(8,128)S(1)}, u32[]{:S(2)}) copy-start(f32[2,64,7]{1,2,0:T(8,128)S(1)} %get-tuple-element.100) | copy-start | bytes 10756
  35.7 7.0 %copy-start.12 = (f32[2,64,7]{1,2,0:T(8,128)}, f32[2,64,7]{1,2,0:T(8,128)S(1)}, u32[]{:S(2)}) copy-start(f32[2,64,7]{1,2,0:T(8,128)S(1)} %get-tuple-element.104) | copy-start | bytes 10756
  35.7 3.1 %copy-start.18 = (f32[2,64]{1,0:T(2,128)S(1)}, f32[2,64]{1,0:T(2,128)}, u32[]{:S(2)}) copy-start(f32[2,64]{1,0:T(2,128)} %reduce_sum.73) | copy-start | bytes 1540
  37.0 0.8 copy-start.1
  37.0 1.8 %copy-start.8 = (f32[2,64,7]{1,2,0:T(8,128)}, f32[2,64,7]{1,2,0:T(8,128)S(1)}, u32[]{:S(2)}) copy-start(f32[2,64,7]{1,2,0:T(8,128)S(1)} %get-tuple-element.263) | copy-start | bytes 10756
  46.7 42.5 %copy-start.9 = (f32[2,64,7]{1,2,0:T(8,128)S(1)}, f32[2,64,7]{1,2,0:T(8,128)}, u32[]{:S(2)}) copy-start(f32[2,64,7]{1,2,0:T(8,128)} %copy-done.8) | copy-start | bytes 10756
  46.7 44.1 %copy-start.11 = (f32[2,64,7]{1,2,0:T(8,128)S(1)}, f32[2,64,7]{1,2,0:T(8,128)}, u32[]{:S(2)}) copy-start(f32[2,64,7]{1,2,0:T(8,128)} %copy-done.10) | copy-start | bytes 10756
  46.7 44.1 %copy-start.13 = (f32[2,64,7]{1,2,0:T(8,128)S(1)}, f32[2,64,7]{1,2,0:T(8,128)}, u32[]{:S(2)}) copy-start(f32[2,64,7]{1,2,0:T(8,128)} %copy-done.12) | copy-start | bytes 10756
  46.7 8.3 %copy-start.7 = (bf16[2,64,7,128]{3,1,2,0:T(8,128)(2,1)S(1)}, bf16[2,64,7,128]{3,1,2,0:T(8,128)(2,1)}, u32[]{:S(2)}) copy-start(bf16[2,64,7,128]{3,1,2,0:T(8,128)(2,1)} %get-tuple-element.436) | copy-start | bytes 688132 | tf_op jit(solution)/shard_map/while
  55.7 0.9 copy-start.14
  55.7 0.9 copy-start.16
  56.5 1.0 copy-start.4
  56.6 1.0 copy-start.15
  56.6 1.0 copy-start.17
  57.6 0.8 copy-start.5
  58.4 8.3 %copy-start.7 = (bf16[2,64,7,128]{3,1,2,0:T(8,128)(2,1)S(1)}, bf16[2,64,7,128]{3,1,2,0:T(8,128)(2,1)}, u32[]{:S(2)}) copy-start(bf16[2,64,7,128]{3,1,2,0:T(8,128)(2,1)} %get-tuple-element.436) | copy-start | bytes 688132 | tf_op jit(solution)/shard_map/while
  67.3 0.9 copy-start.14
  67.3 0.9 copy-start.16
  68.2 1.0 copy-start.4
  68.3 1.0 copy-start.15
  68.3 1.0 copy-start.17
  69.3 0.8 copy-start.5
  70.0 20.7 %collective-permute-start.3 = (f32[2,64,7,128]{3,1,2,0:T(8,128)}, f32[2,64,7,128]{3,1,2,0:T(8,128)}, u32[]{:S(2)}, u32[]{:S(2)}) collective-permute-start(f32[2,64,7,128]{3,1,2,0:T(8,128)} %get-tuple-element.103), channel_id=1, source_target_pairs={{4,0},{8,4},{12,8},{16,12},{20,16},{24,20},{28,24},{32,28},{36,32}... | collective-permute-start | bytes 1376264 | tf_op jit(solution)/shard_map/ppermute | solution.py:18
  82.9 7.4 %collective-permute-start.2 = (f32[2,64,7]{1,2,0:T(8,128)}, f32[2,64,7]{1,2,0:T(8,128)S(1)}, u32[]{:S(2)}, u32[]{:S(2)}) collective-permute-start(f32[2,64,7]{1,2,0:T(8,128)} %get-tuple-element.101), channel_id=1, source_target_pairs={{4,0},{8,4},{12,8},{16,12},{20,16},{24,20},{28,24},{32,28},{36,32}... | collective-permute-start | bytes 10760 | tf_op jit(solution)/shard_map/ppermute | solution.py:18
  85.5 5.2 %collective-permute-start.4 = (f32[2,64,7]{1,2,0:T(8,128)}, f32[2,64,7]{1,2,0:T(8,128)S(1)}, u32[]{:S(2)}, u32[]{:S(2)}) collective-permute-start(f32[2,64,7]{1,2,0:T(8,128)} %get-tuple-element.105), channel_id=1, source_target_pairs={{4,0},{8,4},{12,8},{16,12},{20,16},{24,20},{28,24},{32,28},{36,32}... | collective-permute-start | bytes 10760 | tf_op jit(solution)/shard_map/ppermute | solution.py:18
where the time goes:
time: 124 us; the launch traced here: 123 us
  local copies, waits for them, and re-layouts  31.3 us (25%)
  blocking collectives  26.9 us (22%)
  other arithmetic  25.1 us (20%)
  starting transfers between devices  23.1 us (19%)
  matrix products  14.8 us (12%)
    psum x1, blocking collectives, shards(): lax.psum(jnp.dot(attention, o_weight, preferred_element_type=jnp.float32)...  26.9 us
    ppermute x5, starting transfers between devices, from_behind(): return lax.ppermute(block, axis, route)  23.1 us
    gather x4, local copies, waits for them, and re-layouts, one_request(): pages = jnp.take(pool_slots, table_row, axis=0)  8.31 us
    lt x4, other arithmetic, one_request(): visible = positions < length  5.47 us
    dynamic_slice x4, local copies, waits for them, and re-layouts, sweep_all(): return lax.map(one_request, (query_rows, tables, lengths))  5.16 us
    select_n x8, other arithmetic, one_request(): pages = jnp.take(pool_slots, table_row, axis=0)  5.11 us
    dot_general x4, matrix products, pages_partial(): jnp.einsum('tgd,knd->tgkn', query_rows, pages[..., :head_dim], preferred_...  4.09 us
    while x36, local copies, waits for them, and re-layouts  4.06 us
  transfers between devices with their start and end apart: 5, of which 1 were waited for; matrix products, arithmetic and copies ran while one was open for 28% of the time, Pallas kernels for 0%

commit v1 on v0

v1 whole, which is shorter than its diff:
```python
import math

import jax
import jax.numpy as jnp
from jax import lax
from jax.experimental import pallas as pl
from jax.experimental.pallas import tpu as pltpu
from jax.sharding import PartitionSpec as P

HEAD_SIZE = 128
LOCAL = 2

very_negative = -1e30


def from_behind(block, axis, distance):
    devices = range(lax.axis_size(axis))
    route = [((i - distance) % len(devices), i) for i in devices]
    return lax.ppermute(block, axis, route)


def nt_dot(a, b):
    return lax.dot_general(a, b, (((1,), (1,)), ((), ())), preferred_element_type=jnp.float32)


def attention_kernel(
    table_ref, len_ref, leaf_ref, parents_ref, q_ref, tree_ref, pool_ref, spill_ref,
    att_ref, kept_ref, m_sc, l_sc, a_sc,
):
    n_req, tree_len = parents_ref.shape
    heads = q_ref.shape[1] // HEAD_SIZE
    page_len = pool_ref.shape[1]
    max_pages = table_ref.shape[1]
    spill_slots = spill_ref.shape[0]
    spill_base = pool_ref.shape[0] - spill_slots
    scale = 1.0 / math.sqrt(HEAD_SIZE)
    sub = lax.broadcasted_iota(jnp.int32, (tree_len, tree_len), 0)
    lane = lax.broadcasted_iota(jnp.int32, (tree_len, tree_len), 1)
    eye = (sub == lane).astype(jnp.float32)
    page_lane = lax.broadcasted_iota(jnp.int32, (1, page_len), 1)
    squarings = (tree_len - 1).bit_length()

    for r in range(n_req):
        rows = pl.ds(r * tree_len, tree_len)
        par = parents_ref[r : r + 1, :]
        rt = eye + (sub == par).astype(jnp.float32)
        for _ in range(squarings):
            rb = rt.astype(jnp.bfloat16)
            rt = jnp.minimum(jnp.dot(rb, rb, preferred_element_type=jnp.float32), 1.0)
        reach = nt_dot(eye.astype(jnp.bfloat16), rt.astype(jnp.bfloat16))

        depth = jnp.sum(rt, axis=0, keepdims=True) - 1.0
        leaf = leaf_ref[r]
        kept_mask = jnp.sum(jnp.where(sub == leaf, reach, 0.0), axis=0, keepdims=True)
        selector = jnp.where(
            (sub.astype(jnp.float32) == depth) & (kept_mask > 0.5), 1.0, 0.0
        ).astype(jnp.bfloat16)
        tree_rows = tree_ref[rows, :]
        kept_ref[rows, :] = jnp.dot(
            selector, tree_rows, preferred_element_type=jnp.float32
        ).astype(kept_ref.dtype)

        q = q_ref[rows, :]
        q_all = jnp.concatenate(
            [q[:, g * HEAD_SIZE : (g + 1) * HEAD_SIZE] for g in range(heads)], axis=0
        )

        tree_mask = jnp.concatenate([reach] * heads, axis=0) > 0.5
        s = nt_dot(q_all, tree_rows[:, :HEAD_SIZE]) * scale
        s = jnp.where(tree_mask, s, very_negative)
        m = jnp.max(s, axis=1, keepdims=True)
        w = jnp.where(tree_mask, jnp.exp(s - m), 0.0).astype(jnp.bfloat16)
        m_sc[...] = m
        l_sc[...] = jnp.sum(w.astype(jnp.float32), axis=1, keepdims=True)
        a_sc[...] = jnp.dot(w, tree_rows[:, HEAD_SIZE:], preferred_element_type=jnp.float32)

        length = len_ref[r]
        n_pages = (length + page_len - 1) // page_len
        for k in range(max_pages):

            @pl.when(k < n_pages)
            def _():
                slot = table_ref[r, k]
                if k < LOCAL:
                    page = pool_ref[slot]
                else:
                    page = spill_ref[jnp.clip(slot - spill_base, 0, spill_slots - 1)]
                visible = (k * page_len + page_lane) < length
                ps = nt_dot(q_all, page[:, :HEAD_SIZE]) * scale
                ps = jnp.where(visible, ps, very_negative)
                pm = jnp.max(ps, axis=1, keepdims=True)
                pw = jnp.where(visible, jnp.exp(ps - pm), 0.0).astype(jnp.bfloat16)
                pl_sum = jnp.sum(pw.astype(jnp.float32), axis=1, keepdims=True)
                pa = jnp.dot(pw, page[:, HEAD_SIZE:], preferred_element_type=jnp.float32)
                old_m = m_sc[...]
                new_m = jnp.maximum(old_m, pm)
                f_old = jnp.exp(old_m - new_m)
                f_new = jnp.exp(pm - new_m)
                m_sc[...] = new_m
                l_sc[...] = f_old * l_sc[...] + f_new * pl_sum
                a_sc[...] = f_old * a_sc[...] + f_new * pa

        att = (a_sc[...] / l_sc[...]).astype(att_ref.dtype)
        for g in range(heads):
            att_ref[rows, pl.ds(g * HEAD_SIZE, HEAD_SIZE)] = att[g * tree_len : (g + 1) * tree_len]


def shards(queries, tree_kv, page_pool, page_table, cache_len, parents, accepted, o_weight):
    requests, tree_len = parents.shape
    heads = queries.shape[1] // HEAD_SIZE
    pool_slots = page_pool[:, 0]
    own_slots = requests * LOCAL
    spill = from_behind(pool_slots[own_slots:], "req", -1)
    tree_rows = tree_kv[:, 0, :]
    smem = pl.BlockSpec(memory_space=pltpu.SMEM)
    vmem = pl.BlockSpec(memory_space=pltpu.VMEM)
    attention, kept = pl.pallas_call(
        attention_kernel,
        out_shape=(
            jax.ShapeDtypeStruct(queries.shape, jnp.bfloat16),
            jax.ShapeDtypeStruct(tree_rows.shape, jnp.bfloat16),
        ),
        in_specs=[smem, smem, smem, vmem, vmem, vmem, vmem, vmem],
        out_specs=(vmem, vmem),
        scratch_shapes=[
            pltpu.VMEM((heads * tree_len, 1), jnp.float32),
            pltpu.VMEM((heads * tree_len, 1), jnp.float32),
            pltpu.VMEM((heads * tree_len, HEAD_SIZE), jnp.float32),
        ],
    )(page_table, cache_len, accepted, parents, queries, tree_rows, pool_slots, spill)

    partial = jnp.dot(attention, o_weight, preferred_element_type=jnp.float32)
    parts = lax.axis_size("tp")
    me = lax.axis_index("tp")
    blocks = partial.reshape(parts, partial.shape[0] // parts, partial.shape[1])
    total = blocks[me]
    for shift in range(1, parts):
        outgoing = blocks[(me + shift) % parts]
        route = [(i, (i + shift) % parts) for i in range(parts)]
        total = total + lax.ppermute(outgoing, "tp", route)
    projected = total.astype(jnp.bfloat16)
    return (projected, kept.reshape(kept.shape[0], 1, kept.shape[1]))


def solution(mesh):
    in_specs = (
        P("req", "tp"),
        P("req", "tp", None),
        P("req", "tp", None, None),
        P("req", None),
        P("req"),
        P("req", None),
        P("req"),
        P("tp", None),
    )
    out_specs = (P(("req", "tp"), None), P("req", "tp", None))
    return jax.shard_map(shards, mesh=mesh, in_specs=in_specs, out_specs=out_specs, check_vma=False)
```

time: 124 us -> 59.2 us (0.48)
  the two profiles are of different devices: /device:TPU:8 before, /device:TPU:24 now
where the time goes in v1:
time: 59.2 us; the launch traced here: 58.9 us
  starting transfers between devices  22 us (37%)
  Pallas kernels  15.3 us (26%)
  waiting for transfers between devices  13.5 us (23%)
  local copies, waits for them, and re-layouts  3.85 us (7%)
  other arithmetic  1.85 us (3%)
  matrix products  1.58 us (3%)
  between operations  0.74 us (1%)
    pallas_call x1, Pallas kernels, shards(): pl.pallas_call(attention_kernel, out_shape=(jax.ShapeDtypeStruct(queries....  15.3 us
    ppermute x1, starting transfers between devices, from_behind(): return lax.ppermute(block, axis, route)  13 us
    ppermute x3, starting transfers between devices, shards(): total = total + lax.ppermute(outgoing, 'tp', route)  8.97 us
    ppermute x1, waiting for transfers between devices, from_behind(): return lax.ppermute(block, axis, route)  6.95 us
    ppermute x3, waiting for transfers between devices, shards(): total = total + lax.ppermute(outgoing, 'tp', route)  6.58 us
    slice x1, local copies, waits for them, and re-layouts, shards(): spill = from_behind(pool_slots[own_slots:], 'req', -1)  2.02 us
    convert_element_type x1, other arithmetic, shards(): projected = total.astype(jnp.bfloat16)  1.85 us
    dot_general x1, matrix products, shards(): partial = jnp.dot(attention, o_weight, preferred_element_type=jnp.float32)  1.58 us
  transfers between devices with their start and end apart: 4, of which 3 were waited for; matrix products, arithmetic and copies ran while one was open for 0% of the time, Pallas kernels for 0%

profile of v1, /device:TPU:24, one launch (start us, length us, event | category | flops | bytes accessed | tf_op | source)
XLA Modules:
  0.0 58.9 jit_solution(16143166824858380140)
XLA Ops:
  0.6 0.0 copy-start
  0.6 2.0 %slice_bitcast_fusion = bf16[8,128,256]{2,1,0:T(8,128)(2,1)} fusion(bf16[12,1,128,256]{3,2,0,1:T(8,128)(2,1)} %bitcast.25), kind=kLoop, calls=%fused_computation | loop fusion | bytes 1048576 | tf_op jit(solution)/shard_map/slice | solution.py:113
  2.7 13.0 %collective-permute-start = (bf16[8,128,256]{2,1,0:T(8,128)(2,1)}, bf16[8,128,256]{2,1,0:T(8,128)(2,1)}, u32[]{:S(2)}, u32[]{:S(2)}) collective-permute-start(bf16[8,128,256]{2,1,0:T(8,128)(2,1)} %slice_bitcast_fusion), channel_id=1, source_target_pairs={{4,0},{8,4},{12,8},{16,12},{20,16},{24,20},{28,24},{32,28},{36,32}... | collective-permute-start | bytes 1572872 | tf_op jit(solution)/shard_map/ppermute | solution.py:19
  15.7 6.9 %collective-permute-done.spill_ref = bf16[8,128,256]{2,1,0:T(8,128)(2,1)} collective-permute-done((bf16[8,128,256]{2,1,0:T(8,128)(2,1)}, bf16[8,128,256]{2,1,0:T(8,128)(2,1)}, u32[]{:S(2)}, u32[]{:S(2)}) %collective-permute-start) | collective-permute-done | bytes 524320 | tf_op jit(solution)/shard_map/ppermute | solution.py:19
  22.7 15.3 %shard_map.95 = (bf16[128,896]{1,0:T(8,128)(2,1)}, bf16[128,256]{1,0:T(8,128)(2,1)}) custom-call(s32[2,8]{1,0:T(2,128)} %table_ref.1, s32[2]{0:T(128)} %len_ref.1, s32[2]{0:T(128)} %leaf_ref.1, s32[2,64]{1,0:T(2,128)} %parents_ref.1, bf16[128,896]{1,0:T(8,128)(2,1)} %q_ref.1, bf16[128,256]{1,0:T(8,128)(2,1)} %bitcast.27, bf16[12,128,256]{2,1,0:T(8,128)(2,1)} %bitcast.26, ...), custom_call_target="tpu_custom_call" | custom-call | tf_op jit(solution)/shard_map/pallas_call | solution.py:117
  38.0 0.0 copy-done
  38.0 1.6 %fusion.3 = f32[128,1792]{1,0:T(8,128)S(1)} fusion(bf16[128,896]{1,0:T(8,128)(2,1)} %get-tuple-element.4, bf16[896,1792]{1,0:T(8,128)(2,1)S(1)} %copy-done), kind=kOutput, calls=%fused_computation.8 | convolution fusion | flops 411041792 | bytes 4358144 | tf_op jit(solution)/shard_map/dot_general | solution.py:132
  39.6 0.0 copy-start.1
  39.6 0.9 %copy-done.1 = f32[128,1792]{1,0:T(8,128)} copy-done((f32[128,1792]{1,0:T(8,128)}, f32[128,1792]{1,0:T(8,128)S(1)}, u32[]{:S(2)}) %copy-start.1) | copy-done | bytes 917528
  40.6 0.9 %dynamic-slice_bitcast_fusion.2 = (f32[32,1792]{1,0:T(8,128)}, f32[32,1792]{1,0:T(8,128)}, f32[32,1792]{1,0:T(8,128)}) fusion(f32[4,32,1792]{2,1,0:T(8,128)S(1)} %bitcast.23, s32[]{:T(128)S(6)} %select_n.29, s32[]{:T(128)S(6)} %select_n.33, s32[]{:T(128)S(6)} %select_n.31), kind=kLoop, calls=%fused_computation.7 | loop fusion | bytes 1376268 | tf_op jit(solution)/shard_map/squeeze | solution.py:138
  41.5 2.1 %collective-permute-start.1 = (f32[32,1792]{1,0:T(8,128)}, f32[32,1792]{1,0:T(8,128)S(1)}, u32[]{:S(2)}, u32[]{:S(2)}) collective-permute-start(f32[32,1792]{1,0:T(8,128)} %get-tuple-element.6), channel_id=1, source_target_pairs={{0,1},{1,2},{2,3},{3,0},{4,5},{5,6},{6,7},{7,4},{8,9},{9,10},{10,1... | collective-permute-start | bytes 688136 | tf_op jit(solution)/shard_map/ppermute | solution.py:140
  43.6 3.7 %collective-permute-start.3 = (f32[32,1792]{1,0:T(8,128)}, f32[32,1792]{1,0:T(8,128)}, u32[]{:S(2)}, u32[]{:S(2)}) collective-permute-start(f32[32,1792]{1,0:T(8,128)} %get-tuple-element.7), channel_id=1, source_target_pairs={{0,3},{1,0},{2,1},{3,2},{4,7},{5,4},{6,5},{7,6},{8,11},{9,8},{10,9... | collective-permute-start | bytes 688136 | tf_op jit(solution)/shard_map/ppermute | solution.py:140
  47.3 3.1 %collective-permute-start.2 = (f32[32,1792]{1,0:T(8,128)}, f32[32,1792]{1,0:T(8,128)}, u32[]{:S(2)}, u32[]{:S(2)}) collective-permute-start(f32[32,1792]{1,0:T(8,128)} %get-tuple-element.8), channel_id=1, source_target_pairs={{0,2},{1,3},{2,0},{3,1},{4,6},{5,7},{6,4},{7,5},{8,10},{9,11},{10,... | collective-permute-start | bytes 688136 | tf_op jit(solution)/shard_map/ppermute | solution.py:140
  50.5 0.0 collective-permute-done.1
  50.5 2.6 %collective-permute-done.3 = f32[32,1792]{1,0:T(8,128)} collective-permute-done((f32[32,1792]{1,0:T(8,128)}, f32[32,1792]{1,0:T(8,128)}, u32[]{:S(2)}, u32[]{:S(2)}) %collective-permute-start.3) | collective-permute-done | bytes 229408 | tf_op jit(solution)/shard_map/ppermute | solution.py:140
  53.0 4.0 %collective-permute-done.2 = f32[32,1792]{1,0:T(8,128)} collective-permute-done((f32[32,1792]{1,0:T(8,128)}, f32[32,1792]{1,0:T(8,128)}, u32[]{:S(2)}, u32[]{:S(2)}) %collective-permute-start.2) | collective-permute-done | bytes 229408 | tf_op jit(solution)/shard_map/ppermute | solution.py:140
  57.0 1.8 %fusion.2 = bf16[32,1792]{1,0:T(8,128)(2,1)} fusion(f32[32,1792]{1,0:T(8,128)} %collective-permute-done.3, f32[32,1792]{1,0:T(8,128)} %collective-permute-done.2, f32[32,1792]{1,0:T(8,128)S(1)} %collective-permute-done.1, f32[4,32,1792]{2,1,0:T(8,128)} %bitcast.24, s32[]{:T(128)S(6)} %select_n.27), kind=kLoop, calls=%fused_computation.4 | loop fusion | flops 229376 | bytes 1032196 | tf_op jit(solution)/shard_map/convert_element_type | solution.py:141
Async XLA Ops:
  0.6 37.4 %copy-start = (bf16[896,1792]{1,0:T(8,128)(2,1)S(1)}, bf16[896,1792]{1,0:T(8,128)(2,1)}, u32[]{:S(2)}) copy-start(bf16[896,1792]{1,0:T(8,128)(2,1)} %param.15) | copy-start | bytes 9633796
  2.7 20.0 %collective-permute-start = (bf16[8,128,256]{2,1,0:T(8,128)(2,1)}, bf16[8,128,256]{2,1,0:T(8,128)(2,1)}, u32[]{:S(2)}, u32[]{:S(2)}) collective-permute-start(bf16[8,128,256]{2,1,0:T(8,128)(2,1)} %slice_bitcast_fusion), channel_id=1, source_target_pairs={{4,0},{8,4},{12,8},{16,12},{20,16},{24,20},{28,24},{32,28},{36,32}... | collective-permute-start | bytes 1572872 | tf_op jit(solution)/shard_map/ppermute | solution.py:19
  39.6 0.9 %copy-start.1 = (f32[128,1792]{1,0:T(8,128)}, f32[128,1792]{1,0:T(8,128)S(1)}, u32[]{:S(2)}) copy-start(f32[128,1792]{1,0:T(8,128)S(1)} %fusion.3) | copy-start | bytes 2752516
  41.5 9.0 %collective-permute-start.1 = (f32[32,1792]{1,0:T(8,128)}, f32[32,1792]{1,0:T(8,128)S(1)}, u32[]{:S(2)}, u32[]{:S(2)}) collective-permute-start(f32[32,1792]{1,0:T(8,128)} %get-tuple-element.6), channel_id=1, source_target_pairs={{0,1},{1,2},{2,3},{3,0},{4,5},{5,6},{6,7},{7,4},{8,9},{9,10},{10,1... | collective-permute-start | bytes 688136 | tf_op jit(solution)/shard_map/ppermute | solution.py:140
  43.6 9.4 %collective-permute-start.3 = (f32[32,1792]{1,0:T(8,128)}, f32[32,1792]{1,0:T(8,128)}, u32[]{:S(2)}, u32[]{:S(2)}) collective-permute-start(f32[32,1792]{1,0:T(8,128)} %get-tuple-element.7), channel_id=1, source_target_pairs={{0,3},{1,0},{2,1},{3,2},{4,7},{5,4},{6,5},{7,6},{8,11},{9,8},{10,9... | collective-permute-start | bytes 688136 | tf_op jit(solution)/shard_map/ppermute | solution.py:140
  47.3 9.7 %collective-permute-start.2 = (f32[32,1792]{1,0:T(8,128)}, f32[32,1792]{1,0:T(8,128)}, u32[]{:S(2)}, u32[]{:S(2)}) collective-permute-start(f32[32,1792]{1,0:T(8,128)} %get-tuple-element.8), channel_id=1, source_target_pairs={{0,2},{1,3},{2,0},{3,1},{4,6},{5,7},{6,4},{7,5},{8,10},{9,11},{10,... | collective-permute-start | bytes 688136 | tf_op jit(solution)/shard_map/ppermute | solution.py:140

commit v2 on v1

v2 whole, which is shorter than its diff:
```python
import functools
import math

import jax
import jax.numpy as jnp
from jax import lax
from jax.experimental import pallas as pl
from jax.experimental.pallas import tpu as pltpu
from jax.sharding import PartitionSpec as P

HEAD_SIZE = 128
LOCAL = 2

very_negative = -1e30


def from_behind(block, axis, distance):
    devices = range(lax.axis_size(axis))
    route = [((i - distance) % len(devices), i) for i in devices]
    return lax.ppermute(block, axis, route)


def nt_dot(a, b):
    return lax.dot_general(a, b, (((1,), (1,)), ((), ())), preferred_element_type=jnp.float32)


def stacked_queries(q_ref, rows, heads):
    q = q_ref[rows, :]
    return jnp.concatenate(
        [q[:, g * HEAD_SIZE : (g + 1) * HEAD_SIZE] for g in range(heads)], axis=0
    )


def page_blocks(q_all, pages, first_page, length):
    page_len = pages[0].shape[0]
    keys = jnp.concatenate([page[:, :HEAD_SIZE] for page in pages], axis=0)
    lane = lax.broadcasted_iota(jnp.int32, (1, keys.shape[0]), 1)
    visible = (first_page * page_len + lane) < length
    scores = nt_dot(q_all, keys) * (1.0 / math.sqrt(HEAD_SIZE))
    scores = jnp.where(visible, scores, very_negative)
    blocks = []
    for k, page in enumerate(pages):
        cols = slice(k * page_len, (k + 1) * page_len)
        s = scores[:, cols]
        m = jnp.max(s, axis=1, keepdims=True)
        w = jnp.where(visible[:, cols], jnp.exp(s - m), 0.0).astype(jnp.bfloat16)
        l = jnp.sum(w.astype(jnp.float32), axis=1, keepdims=True)
        a = jnp.dot(w, page[:, HEAD_SIZE:], preferred_element_type=jnp.float32)
        blocks.append((m, l, a))
    return blocks


def merge(blocks):
    top = blocks[0][0]
    for m, _, _ in blocks[1:]:
        top = jnp.maximum(top, m)
    total = None
    accum = None
    for m, l, a in blocks:
        f = jnp.exp(m - top)
        total = f * l if total is None else total + f * l
        accum = f * a if accum is None else accum + f * a
    return top, total, accum


def local_kernel(
    table_ref, len_ref, leaf_ref, parents_ref, q_ref, tree_ref, pool_ref,
    kept_ref, m_ref, l_ref, a_ref,
):
    n_req, tree_len = parents_ref.shape
    heads = q_ref.shape[1] // HEAD_SIZE
    scale = 1.0 / math.sqrt(HEAD_SIZE)
    sub = lax.broadcasted_iota(jnp.int32, (tree_len, tree_len), 0)
    lane = lax.broadcasted_iota(jnp.int32, (tree_len, tree_len), 1)
    eye = (sub == lane).astype(jnp.float32)
    squarings = (tree_len - 1).bit_length()

    for r in range(n_req):
        rows = pl.ds(r * tree_len, tree_len)
        par = parents_ref[r : r + 1, :]
        rt = eye + (sub == par).astype(jnp.float32)
        for _ in range(squarings):
            rb = rt.astype(jnp.bfloat16)
            rt = jnp.minimum(jnp.dot(rb, rb, preferred_element_type=jnp.float32), 1.0)
        reach = nt_dot(eye.astype(jnp.bfloat16), rt.astype(jnp.bfloat16))

        depth = jnp.sum(rt, axis=0, keepdims=True) - 1.0
        leaf = leaf_ref[r]
        kept_mask = jnp.sum(jnp.where(sub == leaf, reach, 0.0), axis=0, keepdims=True)
        selector = jnp.where(
            (sub.astype(jnp.float32) == depth) & (kept_mask > 0.5), 1.0, 0.0
        ).astype(jnp.bfloat16)
        tree_rows = tree_ref[rows, :]
        kept_ref[rows, :] = jnp.dot(
            selector, tree_rows, preferred_element_type=jnp.float32
        ).astype(kept_ref.dtype)

        q_all = stacked_queries(q_ref, rows, heads)
        tree_mask = jnp.concatenate([reach] * heads, axis=0) > 0.5
        s = nt_dot(q_all, tree_rows[:, :HEAD_SIZE]) * scale
        s = jnp.where(tree_mask, s, very_negative)
        m = jnp.max(s, axis=1, keepdims=True)
        w = jnp.where(tree_mask, jnp.exp(s - m), 0.0).astype(jnp.bfloat16)
        l = jnp.sum(w.astype(jnp.float32), axis=1, keepdims=True)
        a = jnp.dot(w, tree_rows[:, HEAD_SIZE:], preferred_element_type=jnp.float32)

        pages = [pool_ref[table_ref[r, k]] for k in range(LOCAL)]
        blocks = [(m, l, a)] + page_blocks(q_all, pages, 0, len_ref[r])
        top, total, accum = merge(blocks)
        m_ref[r] = top
        l_ref[r] = total
        a_ref[r] = accum


def spill_kernel(spill_base, table_ref, len_ref, m_ref, l_ref, a_ref, q_ref, spill_ref, att_ref):
    n_req, tree_len = table_ref.shape[0], q_ref.shape[0] // table_ref.shape[0]
    heads = q_ref.shape[1] // HEAD_SIZE
    max_pages = table_ref.shape[1]
    spill_slots = spill_ref.shape[0]
    for r in range(n_req):
        rows = pl.ds(r * tree_len, tree_len)
        q_all = stacked_queries(q_ref, rows, heads)
        pages = [
            spill_ref[jnp.clip(table_ref[r, k] - spill_base, 0, spill_slots - 1)]
            for k in range(LOCAL, max_pages)
        ]
        blocks = [(m_ref[r], l_ref[r], a_ref[r])] + page_blocks(q_all, pages, LOCAL, len_ref[r])
        _, total, accum = merge(blocks)
        att = (accum / total).astype(att_ref.dtype)
        for g in range(heads):
            att_ref[rows, pl.ds(g * HEAD_SIZE, HEAD_SIZE)] = att[g * tree_len : (g + 1) * tree_len]


def shards(queries, tree_kv, page_pool, page_table, cache_len, parents, accepted, o_weight):
    requests, tree_len = parents.shape
    heads = queries.shape[1] // HEAD_SIZE
    pool_slots = page_pool[:, 0]
    own_slots = requests * LOCAL
    spill = from_behind(pool_slots[own_slots:], "req", -1)
    tree_rows = tree_kv[:, 0, :]
    smem = pl.BlockSpec(memory_space=pltpu.SMEM)
    vmem = pl.BlockSpec(memory_space=pltpu.VMEM)
    stacked = heads * tree_len
    kept, top, total, accum = pl.pallas_call(
        local_kernel,
        out_shape=(
            jax.ShapeDtypeStruct(tree_rows.shape, jnp.bfloat16),
            jax.ShapeDtypeStruct((requests, stacked, 1), jnp.float32),
            jax.ShapeDtypeStruct((requests, stacked, 1), jnp.float32),
            jax.ShapeDtypeStruct((requests, stacked, HEAD_SIZE), jnp.float32),
        ),
        in_specs=[smem, smem, smem, vmem, vmem, vmem, vmem],
        out_specs=(vmem, vmem, vmem, vmem),
    )(page_table, cache_len, accepted, parents, queries, tree_rows, pool_slots)
    attention = pl.pallas_call(
        functools.partial(spill_kernel, own_slots),
        out_shape=jax.ShapeDtypeStruct(queries.shape, jnp.bfloat16),
        in_specs=[smem, smem, vmem, vmem, vmem, vmem, vmem],
        out_specs=vmem,
    )(page_table, cache_len, top, total, accum, queries, spill)

    partial = jnp.dot(attention, o_weight, preferred_element_type=jnp.float32)
    parts = lax.axis_size("tp")
    gathered = lax.all_to_all(partial, "tp", 0, 0, tiled=True)
    blocks = gathered.reshape(parts, partial.shape[0] // parts, partial.shape[1])
    projected = jnp.sum(blocks, axis=0).astype(jnp.bfloat16)
    return (projected, kept.reshape(kept.shape[0], 1, kept.shape[1]))


def solution(mesh):
    in_specs = (
        P("req", "tp"),
        P("req", "tp", None),
        P("req", "tp", None, None),
        P("req", None),
        P("req"),
        P("req", None),
        P("req"),
        P("tp", None),
    )
    out_specs = (P(("req", "tp"), None), P("req", "tp", None))
    return jax.shard_map(shards, mesh=mesh, in_specs=in_specs, out_specs=out_specs, check_vma=False)
```

time: 59.2 us -> 45.6 us (0.77)
  the two profiles are of different devices: /device:TPU:24 before, /device:TPU:8 now
where the time goes in v2:
time: 45.6 us; the launch traced here: 45.3 us
  blocking collectives  13.5 us (30%)
  starting transfers between devices  13 us (29%)
  Pallas kernels  11.1 us (24%)
  local copies, waits for them, and re-layouts  2.05 us (4%)
  other arithmetic  1.91 us (4%)
  matrix products  1.58 us (3%)
  waiting for transfers between devices  1.5 us (3%)
  between operations  0.66 us (1%)
    all_to_all x1, blocking collectives, shards(): gathered = lax.all_to_all(partial, 'tp', 0, 0, tiled=True)  13.5 us
    ppermute x1, starting transfers between devices, from_behind(): return lax.ppermute(block, axis, route)  13 us
    pallas_call x1, Pallas kernels, shards(): pl.pallas_call(functools.partial(spill_kernel, own_slots), out_shape=jax....  5.56 us
    pallas_call x1, Pallas kernels, shards(): pl.pallas_call(local_kernel, out_shape=(jax.ShapeDtypeStruct(tree_rows.sh...  5.49 us
    slice x1, local copies, waits for them, and re-layouts, shards(): spill = from_behind(pool_slots[own_slots:], 'req', -1)  2.04 us
    reduce_sum x1, other arithmetic, shards(): projected = jnp.sum(blocks, axis=0).astype(jnp.bfloat16)  1.91 us
    dot_general x1, matrix products, shards(): partial = jnp.dot(attention, o_weight, preferred_element_type=jnp.float32)  1.58 us
    ppermute x1, waiting for transfers between devices, from_behind(): return lax.ppermute(block, axis, route)  1.5 us
  transfers between devices with their start and end apart: 1, of which 1 were waited for; matrix products, arithmetic and copies ran while one was open for 0% of the time, Pallas kernels for 12%

profile of v2, /device:TPU:8, one launch (start us, length us, event | category | flops | bytes accessed | tf_op | source)
XLA Modules:
  0.0 45.3 jit_solution(10999367496632650816)
XLA Ops:
  0.6 0.0 copy-start
  0.6 2.0 %slice_bitcast_fusion = bf16[8,128,256]{2,1,0:T(8,128)(2,1)} fusion(bf16[12,1,128,256]{3,2,0,1:T(8,128)(2,1)} %bitcast.10), kind=kLoop, calls=%fused_computation | loop fusion | bytes 1048576 | tf_op jit(solution)/shard_map/slice | solution.py:139
  2.7 13.0 %collective-permute-start = (bf16[8,128,256]{2,1,0:T(8,128)(2,1)}, bf16[8,128,256]{2,1,0:T(8,128)(2,1)}, u32[]{:S(2)}, u32[]{:S(2)}) collective-permute-start(bf16[8,128,256]{2,1,0:T(8,128)(2,1)} %slice_bitcast_fusion), channel_id=1, source_target_pairs={{4,0},{8,4},{12,8},{16,12},{20,16},{24,20},{28,24},{32,28},{36,32}... | collective-permute-start | bytes 1572872 | tf_op jit(solution)/shard_map/ppermute | solution.py:20
  15.7 5.5 %shard_map.95 = (bf16[128,256]{1,0:T(8,128)(2,1)}, f32[2,448,1]{2,1,0:T(8,128)}, f32[2,448,1]{2,1,0:T(8,128)}, f32[2,448,128]{2,1,0:T(8,128)}) custom-call(s32[2,8]{1,0:T(2,128)} %table_ref.3, s32[2]{0:T(128)} %len_ref.3, s32[2]{0:T(128)} %leaf_ref.1, s32[2,64]{1,0:T(2,128)} %parents_ref.1, bf16[128,896]{1,0:T(8,128)(2,1)} %q_ref.3, ...), custom_call_target="tpu_custom_call" | custom-call | tf_op jit(solution)/shard_map/pallas_call | solution.py:144
  21.2 1.5 %collective-permute-done.spill_ref = bf16[8,128,256]{2,1,0:T(8,128)(2,1)} collective-permute-done((bf16[8,128,256]{2,1,0:T(8,128)(2,1)}, bf16[8,128,256]{2,1,0:T(8,128)(2,1)}, u32[]{:S(2)}, u32[]{:S(2)}) %collective-permute-start) | collective-permute-done | bytes 524320 | tf_op jit(solution)/shard_map/ppermute | solution.py:20
  22.7 5.6 %shard_map.96 = bf16[128,896]{1,0:T(8,128)(2,1)} custom-call(s32[2,8]{1,0:T(2,128)} %table_ref.3, s32[2]{0:T(128)} %len_ref.3, f32[2,448,1]{2,1,0:T(8,128)} %get-tuple-element.6.m_ref, f32[2,448,1]{2,1,0:T(8,128)} %get-tuple-element.7.l_ref, f32[2,448,128]{2,1,0:T(8,128)} %get-tuple-element.8.a_ref, bf16[128,896]{1,0:T(8,128)(2,1)} %q_ref.3, ...), custom_call_target="tpu_custom_call" | custom-call | tf_op jit(solution)/shard_map/pallas_call | solution.py:155
  28.3 0.0 copy-done
  28.3 1.6 %fusion = f32[128,1792]{1,0:T(8,128)S(1)} fusion(bf16[128,896]{1,0:T(8,128)(2,1)} %shard_map.96, bf16[896,1792]{1,0:T(8,128)(2,1)S(1)} %copy-done), kind=kOutput, calls=%fused_computation.1 | convolution fusion | flops 411041792 | bytes 4358144 | tf_op jit(solution)/shard_map/dot_general | solution.py:162
  29.9 13.5 %all_to_all.9 = f32[4,32,1792]{2,1,0:T(8,128)} all-to-all(f32[4,32,1792]{2,1,0:T(8,128)S(1)} %bitcast.9), channel_id=1, replica_groups=mesh['req'=128,'tp'=4] {'tp'}, dimensions={0} | all-to-all | bytes 1835008 | tf_op jit(solution)/shard_map/all_to_all | solution.py:164
  43.4 1.9 %reduce_sum.9 = bf16[32,1792]{1,0:T(8,128)(2,1)} reduce(f32[4,32,1792]{2,1,0:T(8,128)} %all_to_all.9, f32[]{:T(128)} %constant.0.clone.1), dimensions={0}, to_apply=%region_0.0 | reduce | flops 172032 | bytes 1032196 | tf_op jit(solution)/shard_map/reduce_sum | solution.py:166
Async XLA Ops:
  0.6 27.6 %copy-start = (bf16[896,1792]{1,0:T(8,128)(2,1)S(1)}, bf16[896,1792]{1,0:T(8,128)(2,1)}, u32[]{:S(2)}) copy-start(bf16[896,1792]{1,0:T(8,128)(2,1)} %param.15) | copy-start | bytes 9633796
  2.7 20.0 %collective-permute-start = (bf16[8,128,256]{2,1,0:T(8,128)(2,1)}, bf16[8,128,256]{2,1,0:T(8,128)(2,1)}, u32[]{:S(2)}, u32[]{:S(2)}) collective-permute-start(bf16[8,128,256]{2,1,0:T(8,128)(2,1)} %slice_bitcast_fusion), channel_id=1, source_target_pairs={{4,0},{8,4},{12,8},{16,12},{20,16},{24,20},{28,24},{32,28},{36,32}... | collective-permute-start | bytes 1572872 | tf_op jit(solution)/shard_map/ppermute | solution.py:20

commit v3 on v2

--- a/solution.py
+++ b/solution.py
@@ -161,9 +161,12 @@
 
     partial = jnp.dot(attention, o_weight, preferred_element_type=jnp.float32)
     parts = lax.axis_size("tp")
-    gathered = lax.all_to_all(partial, "tp", 0, 0, tiled=True)
+    gathered = lax.all_to_all(partial.astype(jnp.bfloat16), "tp", 0, 0, tiled=True)
     blocks = gathered.reshape(parts, partial.shape[0] // parts, partial.shape[1])
-    projected = jnp.sum(blocks, axis=0).astype(jnp.bfloat16)
+    summed = blocks[0].astype(jnp.float32)
+    for i in range(1, parts):
+        summed = summed + blocks[i].astype(jnp.float32)
+    projected = summed.astype(jnp.bfloat16)
     return (projected, kept.reshape(kept.shape[0], 1, kept.shape[1]))
 
 

time: 45.6 us -> 41.8 us (0.917)
  blocking collectives: 13.5 us -> 11 us
  other arithmetic: 1.91 us -> 0.7 us
    all_to_all x1, blocking collectives: 13.5 us -> 11 us  [shards(): lax.all_to_all(partial.astype(jnp.bfloat16), 'tp', 0, 0, tiled=True)]
    reduce_sum x1 -> x0, other arithmetic: 1.91 us -> none  [shards(): projected = jnp.sum(blocks, axis=0).astype(jnp.bfloat16)]
    add x0 -> x1, other arithmetic: none -> 0.7 us  [shards(): summed = summed + blocks[i].astype(jnp.float32)]
  transfers between devices with their start and end apart: 1 -> 1, of which waited for: 1 -> 1; matrix products, arithmetic and copies ran while one was open for 0% -> 0% of each run, Pallas kernels for 12% -> 13%
where the time goes in v3:
time: 41.8 us; the launch traced here: 41.5 us
  starting transfers between devices  13 us (31%)
  Pallas kernels  11 us (26%)
  blocking collectives  11 us (26%)
  local copies, waits for them, and re-layouts  2.03 us (5%)
  matrix products  1.58 us (4%)
  waiting for transfers between devices  1.51 us (4%)
  other arithmetic  0.7 us (2%)
  between operations  0.66 us (2%)
    ppermute x1, starting transfers between devices, from_behind(): return lax.ppermute(block, axis, route)  13 us
    all_to_all x1, blocking collectives, shards(): lax.all_to_all(partial.astype(jnp.bfloat16), 'tp', 0, 0, tiled=True)  11 us
    pallas_call x1, Pallas kernels, shards(): pl.pallas_call(functools.partial(spill_kernel, own_slots), out_shape=jax....  5.56 us
    pallas_call x1, Pallas kernels, shards(): pl.pallas_call(local_kernel, out_shape=(jax.ShapeDtypeStruct(tree_rows.sh...  5.48 us
    slice x1, local copies, waits for them, and re-layouts, shards(): spill = from_behind(pool_slots[own_slots:], 'req', -1)  2.02 us
    dot_general x1, matrix products, shards(): partial = jnp.dot(attention, o_weight, preferred_element_type=jnp.float32)  1.58 us
    ppermute x1, waiting for transfers between devices, from_behind(): return lax.ppermute(block, axis, route)  1.51 us
  transfers between devices with their start and end apart: 1, of which 1 were waited for; matrix products, arithmetic and copies ran while one was open for 0% of the time, Pallas kernels for 13%

profile of v3, /device:TPU:8, one launch (start us, length us, event | category | flops | bytes accessed | tf_op | source)
XLA Modules:
  0.0 41.5 jit_solution(2664098979911530018)
XLA Ops:
  0.6 0.0 copy-start
  0.6 2.0 %slice_bitcast_fusion = bf16[8,128,256]{2,1,0:T(8,128)(2,1)} fusion(bf16[12,1,128,256]{3,2,0,1:T(8,128)(2,1)} %bitcast.11), kind=kLoop, calls=%fused_computation.1 | loop fusion | bytes 1048576 | tf_op jit(solution)/shard_map/slice | solution.py:139
  2.7 13.0 %collective-permute-start = (bf16[8,128,256]{2,1,0:T(8,128)(2,1)}, bf16[8,128,256]{2,1,0:T(8,128)(2,1)}, u32[]{:S(2)}, u32[]{:S(2)}) collective-permute-start(bf16[8,128,256]{2,1,0:T(8,128)(2,1)} %slice_bitcast_fusion), channel_id=1, source_target_pairs={{4,0},{8,4},{12,8},{16,12},{20,16},{24,20},{28,24},{32,28},{36,32}... | collective-permute-start | bytes 1572872 | tf_op jit(solution)/shard_map/ppermute | solution.py:20
  15.7 5.5 %shard_map.95 = (bf16[128,256]{1,0:T(8,128)(2,1)}, f32[2,448,1]{2,1,0:T(8,128)}, f32[2,448,1]{2,1,0:T(8,128)}, f32[2,448,128]{2,1,0:T(8,128)}) custom-call(s32[2,8]{1,0:T(2,128)} %table_ref.3, s32[2]{0:T(128)} %len_ref.3, s32[2]{0:T(128)} %leaf_ref.1, s32[2,64]{1,0:T(2,128)} %parents_ref.1, bf16[128,896]{1,0:T(8,128)(2,1)} %q_ref.3, ...), custom_call_target="tpu_custom_call" | custom-call | tf_op jit(solution)/shard_map/pallas_call | solution.py:144
  21.2 1.5 %collective-permute-done.spill_ref = bf16[8,128,256]{2,1,0:T(8,128)(2,1)} collective-permute-done((bf16[8,128,256]{2,1,0:T(8,128)(2,1)}, bf16[8,128,256]{2,1,0:T(8,128)(2,1)}, u32[]{:S(2)}, u32[]{:S(2)}) %collective-permute-start) | collective-permute-done | bytes 524320 | tf_op jit(solution)/shard_map/ppermute | solution.py:20
  22.7 5.6 %shard_map.96 = bf16[128,896]{1,0:T(8,128)(2,1)} custom-call(s32[2,8]{1,0:T(2,128)} %table_ref.3, s32[2]{0:T(128)} %len_ref.3, f32[2,448,1]{2,1,0:T(8,128)} %get-tuple-element.6.m_ref, f32[2,448,1]{2,1,0:T(8,128)} %get-tuple-element.7.l_ref, f32[2,448,128]{2,1,0:T(8,128)} %get-tuple-element.8.a_ref, bf16[128,896]{1,0:T(8,128)(2,1)} %q_ref.3, ...), custom_call_target="tpu_custom_call" | custom-call | tf_op jit(solution)/shard_map/pallas_call | solution.py:155
  28.3 0.0 copy-done
  28.3 1.6 %convolution_convert_fusion = bf16[128,1792]{1,0:T(8,128)(2,1)S(1)} fusion(bf16[128,896]{1,0:T(8,128)(2,1)} %shard_map.96, bf16[896,1792]{1,0:T(8,128)(2,1)S(1)} %copy-done), kind=kOutput, calls=%fused_computation | convolution fusion | flops 411271168 | bytes 3899392 | tf_op jit(solution)/shard_map/dot_general | solution.py:162
  29.8 11.0 %all_to_all.9 = bf16[4,32,1792]{2,1,0:T(8,128)(2,1)S(1)} all-to-all(bf16[4,32,1792]{2,1,0:T(8,128)(2,1)S(1)} %bitcast.13), channel_id=1, replica_groups=mesh['req'=128,'tp'=4] {'tp'}, dimensions={0} | all-to-all | bytes 917504 | tf_op jit(solution)/shard_map/all_to_all | solution.py:164
  40.8 0.7 %fusion = bf16[32,1792]{1,0:T(8,128)(2,1)} fusion(bf16[4,32,1792]{2,1,0:T(8,128)(2,1)S(1)} %all_to_all.9), kind=kLoop, calls=%fused_computation.3 | loop fusion | flops 458752 | bytes 573440 | tf_op jit(solution)/shard_map/add | solution.py:168
Async XLA Ops:
  0.6 27.6 %copy-start = (bf16[896,1792]{1,0:T(8,128)(2,1)S(1)}, bf16[896,1792]{1,0:T(8,128)(2,1)}, u32[]{:S(2)}) copy-start(bf16[896,1792]{1,0:T(8,128)(2,1)} %param.15) | copy-start | bytes 9633796
  2.7 20.0 %collective-permute-start = (bf16[8,128,256]{2,1,0:T(8,128)(2,1)}, bf16[8,128,256]{2,1,0:T(8,128)(2,1)}, u32[]{:S(2)}, u32[]{:S(2)}) collective-permute-start(bf16[8,128,256]{2,1,0:T(8,128)(2,1)} %slice_bitcast_fusion), channel_id=1, source_target_pairs={{4,0},{8,4},{12,8},{16,12},{20,16},{24,20},{28,24},{32,28},{36,32}... | collective-permute-start | bytes 1572872 | tf_op jit(solution)/shard_map/ppermute | solution.py:20

commit v4 on v3

--- a/solution.py
+++ b/solution.py
@@ -65,70 +65,93 @@
 
 def local_kernel(
     table_ref, len_ref, leaf_ref, parents_ref, q_ref, tree_ref, pool_ref,
-    kept_ref, m_ref, l_ref, a_ref,
+    kept_ref, ml_ref, a_ref,
 ):
-    n_req, tree_len = parents_ref.shape
+    nodes = parents_ref.shape[1]
+    n_req = table_ref.shape[0]
+    tree_len = nodes // n_req
     heads = q_ref.shape[1] // HEAD_SIZE
+    stacked = heads * tree_len
     scale = 1.0 / math.sqrt(HEAD_SIZE)
-    sub = lax.broadcasted_iota(jnp.int32, (tree_len, tree_len), 0)
-    lane = lax.broadcasted_iota(jnp.int32, (tree_len, tree_len), 1)
+    sub = lax.broadcasted_iota(jnp.int32, (nodes, nodes), 0)
+    lane = lax.broadcasted_iota(jnp.int32, (nodes, nodes), 1)
     eye = (sub == lane).astype(jnp.float32)
     squarings = (tree_len - 1).bit_length()
 
+    rt = eye + (sub == parents_ref[...]).astype(jnp.float32)
+    for _ in range(squarings):
+        rb = rt.astype(jnp.bfloat16)
+        rt = jnp.minimum(jnp.dot(rb, rb, preferred_element_type=jnp.float32), 1.0)
+    reach = nt_dot(eye.astype(jnp.bfloat16), rt.astype(jnp.bfloat16))
+
+    depth = jnp.sum(rt, axis=0, keepdims=True) - 1.0
+    slot = lax.broadcasted_iota(jnp.int32, (tree_len, nodes), 0).astype(jnp.float32)
+    selectors = []
     for r in range(n_req):
-        rows = pl.ds(r * tree_len, tree_len)
-        par = parents_ref[r : r + 1, :]
-        rt = eye + (sub == par).astype(jnp.float32)
-        for _ in range(squarings):
-            rb = rt.astype(jnp.bfloat16)
-            rt = jnp.minimum(jnp.dot(rb, rb, preferred_element_type=jnp.float32), 1.0)
-        reach = nt_dot(eye.astype(jnp.bfloat16), rt.astype(jnp.bfloat16))
-
-        depth = jnp.sum(rt, axis=0, keepdims=True) - 1.0
-        leaf = leaf_ref[r]
+        leaf = r * tree_len + leaf_ref[r]
         kept_mask = jnp.sum(jnp.where(sub == leaf, reach, 0.0), axis=0, keepdims=True)
-        selector = jnp.where(
-            (sub.astype(jnp.float32) == depth) & (kept_mask > 0.5), 1.0, 0.0
-        ).astype(jnp.bfloat16)
-        tree_rows = tree_ref[rows, :]
-        kept_ref[rows, :] = jnp.dot(
-            selector, tree_rows, preferred_element_type=jnp.float32
-        ).astype(kept_ref.dtype)
-
-        q_all = stacked_queries(q_ref, rows, heads)
-        tree_mask = jnp.concatenate([reach] * heads, axis=0) > 0.5
-        s = nt_dot(q_all, tree_rows[:, :HEAD_SIZE]) * scale
-        s = jnp.where(tree_mask, s, very_negative)
-        m = jnp.max(s, axis=1, keepdims=True)
-        w = jnp.where(tree_mask, jnp.exp(s - m), 0.0).astype(jnp.bfloat16)
-        l = jnp.sum(w.astype(jnp.float32), axis=1, keepdims=True)
-        a = jnp.dot(w, tree_rows[:, HEAD_SIZE:], preferred_element_type=jnp.float32)
-
+        selectors.append(jnp.where((slot == depth) & (kept_mask > 0.5), 1.0, 0.0))
+    selector = jnp.concatenate(selectors, axis=0).astype(jnp.bfloat16)
+    tree_rows = tree_ref[...]
+    kept_ref[...] = jnp.dot(selector, tree_rows, preferred_element_type=jnp.float32).astype(
+        kept_ref.dtype
+    )
+
+    q_all = [stacked_queries(q_ref, pl.ds(r * tree_len, tree_len), heads) for r in range(n_req)]
+    tree_mask = (
+        jnp.concatenate(
+            [reach[r * tree_len : (r + 1) * tree_len] for r in range(n_req) for _ in range(heads)],
+            axis=0,
+        )
+        > 0.5
+    )
+    s = nt_dot(jnp.concatenate(q_all, axis=0), tree_rows[:, :HEAD_SIZE]) * scale
+    s = jnp.where(tree_mask, s, very_negative)
+    m = jnp.max(s, axis=1, keepdims=True)
+    w = jnp.where(tree_mask, jnp.exp(s - m), 0.0).astype(jnp.bfloat16)
+    l = jnp.sum(w.astype(jnp.float32), axis=1, keepdims=True)
+    a = jnp.dot(w, tree_rows[:, HEAD_SIZE:], preferred_element_type=jnp.float32)
+
+    state_lane = lax.broadcasted_iota(jnp.int32, (stacked, HEAD_SIZE), 1)
+    for r in range(n_req):
+        rows = slice(r * stacked, (r + 1) * stacked)
         pages = [pool_ref[table_ref[r, k]] for k in range(LOCAL)]
-        blocks = [(m, l, a)] + page_blocks(q_all, pages, 0, len_ref[r])
+        blocks = [(m[rows], l[rows], a[rows])] + page_blocks(q_all[r], pages, 0, len_ref[r])
         top, total, accum = merge(blocks)
-        m_ref[r] = top
-        l_ref[r] = total
+        ml_ref[r] = jnp.where(state_lane == 0, top, jnp.where(state_lane == 1, total, 0.0))
         a_ref[r] = accum
 
 
-def spill_kernel(spill_base, table_ref, len_ref, m_ref, l_ref, a_ref, q_ref, spill_ref, att_ref):
+def spill_kernel(spill_base, table_ref, len_ref, ml_ref, a_ref, q_ref, spill_ref, att_ref):
     n_req, tree_len = table_ref.shape[0], q_ref.shape[0] // table_ref.shape[0]
     heads = q_ref.shape[1] // HEAD_SIZE
     max_pages = table_ref.shape[1]
     spill_slots = spill_ref.shape[0]
+    page_len = spill_ref.shape[1]
     for r in range(n_req):
         rows = pl.ds(r * tree_len, tree_len)
-        q_all = stacked_queries(q_ref, rows, heads)
-        pages = [
-            spill_ref[jnp.clip(table_ref[r, k] - spill_base, 0, spill_slots - 1)]
-            for k in range(LOCAL, max_pages)
-        ]
-        blocks = [(m_ref[r], l_ref[r], a_ref[r])] + page_blocks(q_all, pages, LOCAL, len_ref[r])
-        _, total, accum = merge(blocks)
-        att = (accum / total).astype(att_ref.dtype)
-        for g in range(heads):
-            att_ref[rows, pl.ds(g * HEAD_SIZE, HEAD_SIZE)] = att[g * tree_len : (g + 1) * tree_len]
+        length = len_ref[r]
+
+        def write(att):
+            for g in range(heads):
+                att_ref[rows, pl.ds(g * HEAD_SIZE, HEAD_SIZE)] = att[g * tree_len : (g + 1) * tree_len]
+
+        @pl.when(length > LOCAL * page_len)
+        def _():
+            q_all = stacked_queries(q_ref, rows, heads)
+            pages = [
+                spill_ref[jnp.clip(table_ref[r, k] - spill_base, 0, spill_slots - 1)]
+                for k in range(LOCAL, max_pages)
+            ]
+            ml = ml_ref[r]
+            state = (ml[:, 0:1], ml[:, 1:2], a_ref[r])
+            _, total, accum = merge([state] + page_blocks(q_all, pages, LOCAL, length))
+            write((accum / total).astype(att_ref.dtype))
+
+        @pl.when(length <= LOCAL * page_len)
+        def _():
+            ml = ml_ref[r]
+            write((a_ref[r] / ml[:, 1:2]).astype(att_ref.dtype))
 
 
 def shards(queries, tree_kv, page_pool, page_table, cache_len, parents, accepted, o_weight):
@@ -141,23 +164,24 @@
     smem = pl.BlockSpec(memory_space=pltpu.SMEM)
     vmem = pl.BlockSpec(memory_space=pltpu.VMEM)
     stacked = heads * tree_len
-    kept, top, total, accum = pl.pallas_call(
+    offsets = (jnp.arange(requests, dtype=jnp.int32) * tree_len)[:, None]
+    parent_ids = jnp.where(parents >= 0, parents + offsets, -1).reshape(1, requests * tree_len)
+    kept, packed, accum = pl.pallas_call(
         local_kernel,
         out_shape=(
             jax.ShapeDtypeStruct(tree_rows.shape, jnp.bfloat16),
-            jax.ShapeDtypeStruct((requests, stacked, 1), jnp.float32),
-            jax.ShapeDtypeStruct((requests, stacked, 1), jnp.float32),
+            jax.ShapeDtypeStruct((requests, stacked, HEAD_SIZE), jnp.float32),
             jax.ShapeDtypeStruct((requests, stacked, HEAD_SIZE), jnp.float32),
         ),
         in_specs=[smem, smem, smem, vmem, vmem, vmem, vmem],
-        out_specs=(vmem, vmem, vmem, vmem),
-    )(page_table, cache_len, accepted, parents, queries, tree_rows, pool_slots)
+        out_specs=(vmem, vmem, vmem),
+    )(page_table, cache_len, accepted, parent_ids, queries, tree_rows, pool_slots)
     attention = pl.pallas_call(
         functools.partial(spill_kernel, own_slots),
         out_shape=jax.ShapeDtypeStruct(queries.shape, jnp.bfloat16),
-        in_specs=[smem, smem, vmem, vmem, vmem, vmem, vmem],
+        in_specs=[smem, smem, vmem, vmem, vmem, vmem],
         out_specs=vmem,
-    )(page_table, cache_len, top, total, accum, queries, spill)
+    )(page_table, cache_len, packed, accum, queries, spill)
 
     partial = jnp.dot(attention, o_weight, preferred_element_type=jnp.float32)
     parts = lax.axis_size("tp")

time: 41.8 us -> 41.8 us (level)
  Pallas kernels: 11 us -> 10 us
  other arithmetic: 0.7 us -> 1.46 us
  local copies, waits for them, and re-layouts: 2.03 us -> 2.63 us
    pallas_call x1, Pallas kernels: 5.48 us -> 4.48 us  [shards(): pl.pallas_call(local_kernel, out_shape=(jax.ShapeDtypeStruct(tree_rows.sh...]
    select_n x0 -> x1, other arithmetic: none -> 0.75 us  [shards(): jnp.where(parents >= 0, parents + offsets, -1)]
    reshape x0 -> x1, local copies, waits for them, and re-layouts: none -> 0.59 us  [shards(): jnp.where(parents >= 0, parents + offsets, -1)]
  transfers between devices with their start and end apart: 1 -> 1, of which waited for: 1 -> 1; matrix products, arithmetic and copies ran while one was open for 0% -> 3% of each run, Pallas kernels for 13% -> 11%
where the time goes in v4:
time: 41.8 us; the launch traced here: 41.5 us
  starting transfers between devices  13 us (31%)
  blocking collectives  11 us (26%)
  Pallas kernels  10 us (24%)
  local copies, waits for them, and re-layouts  2.63 us (6%)
  matrix products  1.58 us (4%)
  other arithmetic  1.46 us (3%)
  waiting for transfers between devices  1.15 us (3%)
  between operations  0.66 us (2%)
    ppermute x1, starting transfers between devices, from_behind(): return lax.ppermute(block, axis, route)  13 us
    all_to_all x1, blocking collectives, shards(): lax.all_to_all(partial.astype(jnp.bfloat16), 'tp', 0, 0, tiled=True)  11 us
    pallas_call x1, Pallas kernels, shards(): pl.pallas_call(functools.partial(spill_kernel, own_slots), out_shape=jax....  5.53 us
    pallas_call x1, Pallas kernels, shards(): pl.pallas_call(local_kernel, out_shape=(jax.ShapeDtypeStruct(tree_rows.sh...  4.48 us
    slice x1, local copies, waits for them, and re-layouts, shards(): spill = from_behind(pool_slots[own_slots:], 'req', -1)  2.02 us
    dot_general x1, matrix products, shards(): partial = jnp.dot(attention, o_weight, preferred_element_type=jnp.float32)  1.58 us
    ppermute x1, waiting for transfers between devices, from_behind(): return lax.ppermute(block, axis, route)  1.15 us
  transfers between devices with their start and end apart: 1, of which 1 were waited for; matrix products, arithmetic and copies ran while one was open for 3% of the time, Pallas kernels for 11%

profile of v4, /device:TPU:8, one launch (start us, length us, event | category | flops | bytes accessed | tf_op | source)
XLA Modules:
  0.0 41.5 jit_solution(473497280222273794)
XLA Ops:
  0.6 0.0 copy-start
  0.6 2.0 %slice_bitcast_fusion = bf16[8,128,256]{2,1,0:T(8,128)(2,1)} fusion(bf16[12,1,128,256]{3,2,0,1:T(8,128)(2,1)} %bitcast.11), kind=kLoop, calls=%fused_computation.1 | loop fusion | bytes 1048576 | tf_op jit(solution)/shard_map/slice | solution.py:162
  2.7 13.0 %collective-permute-start = (bf16[8,128,256]{2,1,0:T(8,128)(2,1)}, bf16[8,128,256]{2,1,0:T(8,128)(2,1)}, u32[]{:S(2)}, u32[]{:S(2)}) collective-permute-start(bf16[8,128,256]{2,1,0:T(8,128)(2,1)} %slice_bitcast_fusion), channel_id=1, source_target_pairs={{4,0},{8,4},{12,8},{16,12},{20,16},{24,20},{28,24},{32,28},{36,32}... | collective-permute-start | bytes 1572872 | tf_op jit(solution)/shard_map/ppermute | solution.py:20
  15.7 0.8 %compare_select_fusion = s32[2,64]{1,0:T(2,128)S(1)} fusion(s32[2,64]{1,0:T(2,128)} %param.13, s32[2]{0:T(128)S(1)} %iota_multiply_fusion), kind=kLoop, calls=%fused_computation.4 | loop fusion | flops 384 | bytes 1032 | tf_op jit(solution)/shard_map/jit(_where)/select_n | solution.py:168
  16.5 0.6 %reshape.38.parents_ref = s32[1,128]{1,0:T(1,128)} reshape(s32[2,64]{1,0:T(2,128)S(1)} %compare_select_fusion) | data formatting | bytes 1024 | tf_op jit(solution)/shard_map/reshape | solution.py:168
  17.1 4.5 %shard_map.95 = (bf16[128,256]{1,0:T(8,128)(2,1)}, f32[2,448,128]{2,1,0:T(8,128)}, f32[2,448,128]{2,1,0:T(8,128)}) custom-call(s32[2,8]{1,0:T(2,128)} %table_ref.3, s32[2]{0:T(128)} %len_ref.3, s32[2]{0:T(128)} %leaf_ref.1, s32[1,128]{1,0:T(1,128)} %reshape.38.parents_ref, bf16[128,896]{1,0:T(8,128)(2,1)} %q_ref.3, bf16[128,256]{1,0:T(8,128)(2,1)} %bitcast.14, ...), custom_call_target="tpu_custom_call" | custom-call | tf_op jit(solution)/shard_map/pallas_call | solution.py:169
  21.5 1.2 %collective-permute-done.spill_ref = bf16[8,128,256]{2,1,0:T(8,128)(2,1)} collective-permute-done((bf16[8,128,256]{2,1,0:T(8,128)(2,1)}, bf16[8,128,256]{2,1,0:T(8,128)(2,1)}, u32[]{:S(2)}, u32[]{:S(2)}) %collective-permute-start) | collective-permute-done | bytes 524320 | tf_op jit(solution)/shard_map/ppermute | solution.py:20
  22.7 5.5 %shard_map.96 = bf16[128,896]{1,0:T(8,128)(2,1)} custom-call(s32[2,8]{1,0:T(2,128)} %table_ref.3, s32[2]{0:T(128)} %len_ref.3, f32[2,448,128]{2,1,0:T(8,128)} %get-tuple-element.5.ml_ref, f32[2,448,128]{2,1,0:T(8,128)} %get-tuple-element.6.a_ref, bf16[128,896]{1,0:T(8,128)(2,1)} %q_ref.3, bf16[8,128,256]{2,1,0:T(8,128)(2,1)} %collective-permute-done.spill_ref), custom_call_target="tpu_custom_call" | custom-call | tf_op jit(solution)/shard_map/pallas_call | solution.py:179
  28.2 0.0 copy-done
  28.2 1.6 %convolution_convert_fusion = bf16[128,1792]{1,0:T(8,128)(2,1)S(1)} fusion(bf16[128,896]{1,0:T(8,128)(2,1)} %shard_map.96, bf16[896,1792]{1,0:T(8,128)(2,1)S(1)} %copy-done), kind=kOutput, calls=%fused_computation | convolution fusion | flops 411271168 | bytes 3899392 | tf_op jit(solution)/shard_map/dot_general | solution.py:186
  29.8 11.0 %all_to_all.9 = bf16[4,32,1792]{2,1,0:T(8,128)(2,1)S(1)} all-to-all(bf16[4,32,1792]{2,1,0:T(8,128)(2,1)S(1)} %bitcast.13), channel_id=1, replica_groups=mesh['req'=128,'tp'=4] {'tp'}, dimensions={0} | all-to-all | bytes 917504 | tf_op jit(solution)/shard_map/all_to_all | solution.py:188
  40.8 0.7 %fusion = bf16[32,1792]{1,0:T(8,128)(2,1)} fusion(bf16[4,32,1792]{2,1,0:T(8,128)(2,1)S(1)} %all_to_all.9), kind=kLoop, calls=%fused_computation.3 | loop fusion | flops 458752 | bytes 573440 | tf_op jit(solution)/shard_map/add | solution.py:192
  (1 shorter events, 0.0 us)
Async XLA Ops:
  0.6 27.6 %copy-start = (bf16[896,1792]{1,0:T(8,128)(2,1)S(1)}, bf16[896,1792]{1,0:T(8,128)(2,1)}, u32[]{:S(2)}) copy-start(bf16[896,1792]{1,0:T(8,128)(2,1)} %param.15) | copy-start | bytes 9633796
  2.7 20.0 %collective-permute-start = (bf16[8,128,256]{2,1,0:T(8,128)(2,1)}, bf16[8,128,256]{2,1,0:T(8,128)(2,1)}, u32[]{:S(2)}, u32[]{:S(2)}) collective-permute-start(bf16[8,128,256]{2,1,0:T(8,128)(2,1)} %slice_bitcast_fusion), channel_id=1, source_target_pairs={{4,0},{8,4},{12,8},{16,12},{20,16},{24,20},{28,24},{32,28},{36,32}... | collective-permute-start | bytes 1572872 | tf_op jit(solution)/shard_map/ppermute | solution.py:20

commit v5 on v4

--- a/solution.py
+++ b/solution.py
@@ -8,16 +8,11 @@
 from jax.experimental.pallas import tpu as pltpu
 from jax.sharding import PartitionSpec as P
 
+
 HEAD_SIZE = 128
 LOCAL = 2
 
 very_negative = -1e30
-
-
-def from_behind(block, axis, distance):
-    devices = range(lax.axis_size(axis))
-    route = [((i - distance) % len(devices), i) for i in devices]
-    return lax.ppermute(block, axis, route)
 
 
 def nt_dot(a, b):
@@ -67,9 +62,8 @@
     table_ref, len_ref, leaf_ref, parents_ref, q_ref, tree_ref, pool_ref,
     kept_ref, ml_ref, a_ref,
 ):
-    nodes = parents_ref.shape[1]
-    n_req = table_ref.shape[0]
-    tree_len = nodes // n_req
+    n_req, tree_len = parents_ref.shape
+    nodes = n_req * tree_len
     heads = q_ref.shape[1] // HEAD_SIZE
     stacked = heads * tree_len
     scale = 1.0 / math.sqrt(HEAD_SIZE)
@@ -78,7 +72,19 @@
     eye = (sub == lane).astype(jnp.float32)
     squarings = (tree_len - 1).bit_length()
 
-    rt = eye + (sub == parents_ref[...]).astype(jnp.float32)
+    parents = parents_ref[...].astype(jnp.float32)
+    first = lax.broadcasted_iota(jnp.int32, parents.shape, 0).astype(jnp.float32) * tree_len
+    parents = jnp.where(parents >= 0.0, parents + first, -1.0).astype(jnp.bfloat16)
+    node = lax.broadcasted_iota(jnp.int32, (tree_len, nodes), 0)
+    column = lax.broadcasted_iota(jnp.int32, (tree_len, nodes), 1)
+    parent_row = None
+    for r in range(n_req):
+        place = (column == node + r * tree_len).astype(jnp.bfloat16)
+        lhs = jnp.broadcast_to(parents[r : r + 1], (16, tree_len))
+        placed = jnp.dot(lhs, place, preferred_element_type=jnp.float32)[0:1]
+        parent_row = placed if parent_row is None else parent_row + placed
+
+    rt = eye + (sub.astype(jnp.float32) == parent_row).astype(jnp.float32)
     for _ in range(squarings):
         rb = rt.astype(jnp.bfloat16)
         rt = jnp.minimum(jnp.dot(rb, rb, preferred_element_type=jnp.float32), 1.0)
@@ -122,7 +128,9 @@
         a_ref[r] = accum
 
 
-def spill_kernel(spill_base, table_ref, len_ref, ml_ref, a_ref, q_ref, spill_ref, att_ref):
+def spill_kernel(
+    spill_base, table_ref, len_ref, flag_ref, ml_ref, a_ref, q_ref, spill_ref, far_ref, att_ref
+):
     n_req, tree_len = table_ref.shape[0], q_ref.shape[0] // table_ref.shape[0]
     heads = q_ref.shape[1] // HEAD_SIZE
     max_pages = table_ref.shape[1]
@@ -139,10 +147,11 @@
         @pl.when(length > LOCAL * page_len)
         def _():
             q_all = stacked_queries(q_ref, rows, heads)
-            pages = [
-                spill_ref[jnp.clip(table_ref[r, k] - spill_base, 0, spill_slots - 1)]
-                for k in range(LOCAL, max_pages)
-            ]
+            far = flag_ref[0] > 0
+            pages = []
+            for k in range(LOCAL, max_pages):
+                index = jnp.clip(table_ref[r, k] - spill_base, 0, spill_slots - 1)
+                pages.append(jnp.where(far, far_ref[index], spill_ref[index]))
             ml = ml_ref[r]
             state = (ml[:, 0:1], ml[:, 1:2], a_ref[r])
             _, total, accum = merge([state] + page_blocks(q_all, pages, LOCAL, length))
@@ -154,19 +163,19 @@
             write((a_ref[r] / ml[:, 1:2]).astype(att_ref.dtype))
 
 
-def shards(queries, tree_kv, page_pool, page_table, cache_len, parents, accepted, o_weight):
+def step(queries, tree_kv, page_pool, page_table, cache_len, parents, accepted, o_weight):
     requests, tree_len = parents.shape
     heads = queries.shape[1] // HEAD_SIZE
     pool_slots = page_pool[:, 0]
     own_slots = requests * LOCAL
-    spill = from_behind(pool_slots[own_slots:], "req", -1)
+    ring = lax.axis_size("req")
+    spill_source = pool_slots[own_slots:]
+    spill = lax.ppermute(spill_source, "req", [(i + 1, i) for i in range(ring - 1)])
     tree_rows = tree_kv[:, 0, :]
     smem = pl.BlockSpec(memory_space=pltpu.SMEM)
     vmem = pl.BlockSpec(memory_space=pltpu.VMEM)
     stacked = heads * tree_len
-    offsets = (jnp.arange(requests, dtype=jnp.int32) * tree_len)[:, None]
-    parent_ids = jnp.where(parents >= 0, parents + offsets, -1).reshape(1, requests * tree_len)
-    kept, packed, accum = pl.pallas_call(
+    local_call = pl.pallas_call(
         local_kernel,
         out_shape=(
             jax.ShapeDtypeStruct(tree_rows.shape, jnp.bfloat16),
@@ -175,13 +184,19 @@
         ),
         in_specs=[smem, smem, smem, vmem, vmem, vmem, vmem],
         out_specs=(vmem, vmem, vmem),
-    )(page_table, cache_len, accepted, parent_ids, queries, tree_rows, pool_slots)
+    )
+    kept, packed, accum = local_call(
+        page_table, cache_len, accepted, parents, queries, tree_rows, pool_slots
+    )
+    kept, packed, accum, spill_source = lax.optimization_barrier((kept, packed, accum, spill_source))
+    far_spill = lax.ppermute(spill_source, "req", [(0, ring - 1)])
+    far_flag = (lax.axis_index("req") == ring - 1).astype(jnp.int32).reshape(1)
     attention = pl.pallas_call(
         functools.partial(spill_kernel, own_slots),
         out_shape=jax.ShapeDtypeStruct(queries.shape, jnp.bfloat16),
-        in_specs=[smem, smem, vmem, vmem, vmem, vmem],
+        in_specs=[smem, smem, smem, vmem, vmem, vmem, vmem, vmem],
         out_specs=vmem,
-    )(page_table, cache_len, packed, accum, queries, spill)
+    )(page_table, cache_len, far_flag, packed, accum, queries, spill, far_spill)
 
     partial = jnp.dot(attention, o_weight, preferred_element_type=jnp.float32)
     parts = lax.axis_size("tp")
@@ -206,4 +221,4 @@
         P("tp", None),
     )
     out_specs = (P(("req", "tp"), None), P("req", "tp", None))
-    return jax.shard_map(shards, mesh=mesh, in_specs=in_specs, out_specs=out_specs, check_vma=False)
+    return jax.shard_map(step, mesh=mesh, in_specs=in_specs, out_specs=out_specs, check_vma=False)

time: 41.8 us -> 46.5 us (1.11)
  waiting for transfers between devices: 1.15 us -> 4.92 us
  starting transfers between devices: 13 us -> 15.1 us
  other arithmetic: 1.46 us -> 0.7 us
  local copies, waits for them, and re-layouts: 2.63 us -> 2.05 us
    ppermute x1 -> x2, waiting for transfers between devices: 1.15 us -> 4.92 us  [the longest x1 4.92 us: step(): far_spill = lax.ppermute(spill_source, 'req', [(0, ring - 1)])]
    ppermute x1 -> x2, starting transfers between devices: 13 us -> 15.1 us  [the longest x1 13.8 us: step(): far_spill = lax.ppermute(spill_source, 'req', [(0, ring - 1)])]
    select_n x1 -> x0, other arithmetic: 0.75 us -> none  [shards(): jnp.where(parents >= 0, parents + offsets, -1)]
    reshape x1 -> x0, local copies, waits for them, and re-layouts: 0.59 us -> none  [shards(): jnp.where(parents >= 0, parents + offsets, -1)]
  transfers between devices with their start and end apart: 1 -> 2, of which waited for: 1 -> 1; matrix products, arithmetic and copies ran while one was open for 3% -> 0% of each run, Pallas kernels for 11% -> 0%
where the time goes in v5:
time: 46.5 us; the launch traced here: 46.2 us
  starting transfers between devices  15.1 us (32%)
  blocking collectives  11 us (24%)
  Pallas kernels  10.2 us (22%)
  waiting for transfers between devices  4.92 us (11%)
  local copies, waits for them, and re-layouts  2.05 us (4%)
  matrix products  1.58 us (3%)
  other arithmetic  0.7 us (2%)
  between operations  0.66 us (1%)
    ppermute x1, starting transfers between devices, step(): far_spill = lax.ppermute(spill_source, 'req', [(0, ring - 1)])  13.8 us
    all_to_all x1, blocking collectives, step(): lax.all_to_all(partial.astype(jnp.bfloat16), 'tp', 0, 0, tiled=True)  11 us
    pallas_call x1, Pallas kernels, step(): pl.pallas_call(functools.partial(spill_kernel, own_slots), out_shape=jax....  5.71 us
    ppermute x1, waiting for transfers between devices, step(): far_spill = lax.ppermute(spill_source, 'req', [(0, ring - 1)])  4.92 us
    pallas_call x1, Pallas kernels, step(): local_call(page_table, cache_len, accepted, parents, queries, tree_rows,...  4.54 us
    slice x1, local copies, waits for them, and re-layouts, step(): spill_source = pool_slots[own_slots:]  2.04 us
    dot_general x1, matrix products, step(): partial = jnp.dot(attention, o_weight, preferred_element_type=jnp.float32)  1.58 us
    ppermute x1, starting transfers between devices, step(): lax.ppermute(spill_source, 'req', [(i + 1, i) for i in range(ring - 1)])  1.28 us
  transfers between devices with their start and end apart: 2, of which 1 were waited for; matrix products, arithmetic and copies ran while one was open for 0% of the time, Pallas kernels for 0%

profile of v5, /device:TPU:8, one launch (start us, length us, event | category | flops | bytes accessed | tf_op | source)
XLA Modules:
  0.0 46.2 jit_solution(6413746984090277049)
XLA Ops:
  0.6 0.0 copy-start
  0.6 2.0 %slice_bitcast_fusion = bf16[8,128,256]{2,1,0:T(8,128)(2,1)} fusion(bf16[12,1,128,256]{3,2,0,1:T(8,128)(2,1)} %bitcast.12), kind=kLoop, calls=%fused_computation.1 | loop fusion | bytes 1048576 | tf_op jit(solution)/shard_map/slice | solution.py:172
  2.7 4.5 %shard_map.95 = (bf16[128,256]{1,0:T(8,128)(2,1)}, f32[2,448,128]{2,1,0:T(8,128)}, f32[2,448,128]{2,1,0:T(8,128)}) custom-call(s32[2,8]{1,0:T(2,128)} %table_ref.3, s32[2]{0:T(128)} %len_ref.3, s32[2]{0:T(128)} %leaf_ref.1, s32[2,64]{1,0:T(2,128)} %parents_ref.1, bf16[128,896]{1,0:T(8,128)(2,1)} %q_ref.3, bf16[128,256]{1,0:T(8,128)(2,1)} %bitcast.15, ...), custom_call_target="tpu_custom_call" | custom-call | tf_op jit(solution)/shard_map/pallas_call | solution.py:188
  7.2 13.8 %collective-permute-start.1 = (bf16[8,128,256]{2,1,0:T(8,128)(2,1)}, bf16[8,128,256]{2,1,0:T(8,128)(2,1)}, u32[]{:S(2)}, u32[]{:S(2)}) collective-permute-start(bf16[8,128,256]{2,1,0:T(8,128)(2,1)} %slice_bitcast_fusion), channel_id=1, source_target_pairs={{0,508},{1,509},{2,510},{3,511}} | collective-permute-start | bytes 1572872 | tf_op jit(solution)/shard_map/ppermute | solution.py:192
  21.0 1.3 %collective-permute-start = (bf16[8,128,256]{2,1,0:T(8,128)(2,1)}, bf16[8,128,256]{2,1,0:T(8,128)(2,1)}, u32[]{:S(2)}, u32[]{:S(2)}) collective-permute-start(bf16[8,128,256]{2,1,0:T(8,128)(2,1)} %slice_bitcast_fusion), channel_id=1, source_target_pairs={{4,0},{8,4},{12,8},{16,12},{20,16},{24,20},{28,24},{32,28},{36,32}... | collective-permute-start | bytes 1572872 | tf_op jit(solution)/shard_map/ppermute | solution.py:173
  22.3 4.9 %collective-permute-done.1.far_ref = bf16[8,128,256]{2,1,0:T(8,128)(2,1)} collective-permute-done((bf16[8,128,256]{2,1,0:T(8,128)(2,1)}, bf16[8,128,256]{2,1,0:T(8,128)(2,1)}, u32[]{:S(2)}, u32[]{:S(2)}) %collective-permute-start.1) | collective-permute-done | bytes 524320 | tf_op jit(solution)/shard_map/ppermute | solution.py:192
  27.2 0.0 collective-permute-done.spill_ref
  27.2 5.7 %shard_map.96 = bf16[128,896]{1,0:T(8,128)(2,1)} custom-call(s32[2,8]{1,0:T(2,128)} %table_ref.3, s32[2]{0:T(128)} %len_ref.3, s32[1]{0:T(128)} %bitcast.flag_ref, f32[2,448,128]{2,1,0:T(8,128)} %get-tuple-element.12.ml_ref, f32[2,448,128]{2,1,0:T(8,128)} %get-tuple-element.13.a_ref, bf16[128,896]{1,0:T(8,128)(2,1)} %q_ref.3, ...), custom_call_target="tpu_custom_call" | custom-call | tf_op jit(solution)/shard_map/pallas_call | solution.py:194
  33.0 0.0 copy-done
  33.0 1.6 %convolution_convert_fusion = bf16[128,1792]{1,0:T(8,128)(2,1)S(1)} fusion(bf16[128,896]{1,0:T(8,128)(2,1)} %shard_map.96, bf16[896,1792]{1,0:T(8,128)(2,1)S(1)} %copy-done), kind=kOutput, calls=%fused_computation | convolution fusion | flops 411271168 | bytes 3899392 | tf_op jit(solution)/shard_map/dot_general | solution.py:201
  34.6 11.0 %all_to_all.9 = bf16[4,32,1792]{2,1,0:T(8,128)(2,1)S(1)} all-to-all(bf16[4,32,1792]{2,1,0:T(8,128)(2,1)S(1)} %bitcast.14), channel_id=1, replica_groups=mesh['req'=128,'tp'=4] {'tp'}, dimensions={0} | all-to-all | bytes 917504 | tf_op jit(solution)/shard_map/all_to_all | solution.py:203
  45.5 0.7 %fusion = bf16[32,1792]{1,0:T(8,128)(2,1)} fusion(bf16[4,32,1792]{2,1,0:T(8,128)(2,1)S(1)} %all_to_all.9), kind=kLoop, calls=%fused_computation.3 | loop fusion | flops 458752 | bytes 573440 | tf_op jit(solution)/shard_map/add | solution.py:207
Async XLA Ops:
  0.6 32.3 %copy-start = (bf16[896,1792]{1,0:T(8,128)(2,1)S(1)}, bf16[896,1792]{1,0:T(8,128)(2,1)}, u32[]{:S(2)}) copy-start(bf16[896,1792]{1,0:T(8,128)(2,1)} %param.15) | copy-start | bytes 9633796
  7.2 20.0 %collective-permute-start.1 = (bf16[8,128,256]{2,1,0:T(8,128)(2,1)}, bf16[8,128,256]{2,1,0:T(8,128)(2,1)}, u32[]{:S(2)}, u32[]{:S(2)}) collective-permute-start(bf16[8,128,256]{2,1,0:T(8,128)(2,1)} %slice_bitcast_fusion), channel_id=1, source_target_pairs={{0,508},{1,509},{2,510},{3,511}} | collective-permute-start | bytes 1572872 | tf_op jit(solution)/shard_map/ppermute | solution.py:192
  21.0 6.2 %collective-permute-start = (bf16[8,128,256]{2,1,0:T(8,128)(2,1)}, bf16[8,128,256]{2,1,0:T(8,128)(2,1)}, u32[]{:S(2)}, u32[]{:S(2)}) collective-permute-start(bf16[8,128,256]{2,1,0:T(8,128)(2,1)} %slice_bitcast_fusion), channel_id=1, source_target_pairs={{4,0},{8,4},{12,8},{16,12},{20,16},{24,20},{28,24},{32,28},{36,32}... | collective-permute-start | bytes 1572872 | tf_op jit(solution)/shard_map/ppermute | solution.py:173

commit v6 on v5

--- a/solution.py
+++ b/solution.py
@@ -7,7 +7,6 @@
 from jax.experimental import pallas as pl
 from jax.experimental.pallas import tpu as pltpu
 from jax.sharding import PartitionSpec as P
-
 
 HEAD_SIZE = 128
 LOCAL = 2
@@ -128,9 +127,7 @@
         a_ref[r] = accum
 
 
-def spill_kernel(
-    spill_base, table_ref, len_ref, flag_ref, ml_ref, a_ref, q_ref, spill_ref, far_ref, att_ref
-):
+def spill_kernel(spill_base, table_ref, len_ref, ml_ref, a_ref, q_ref, spill_ref, att_ref):
     n_req, tree_len = table_ref.shape[0], q_ref.shape[0] // table_ref.shape[0]
     heads = q_ref.shape[1] // HEAD_SIZE
     max_pages = table_ref.shape[1]
@@ -147,11 +144,10 @@
         @pl.when(length > LOCAL * page_len)
         def _():
             q_all = stacked_queries(q_ref, rows, heads)
-            far = flag_ref[0] > 0
-            pages = []
-            for k in range(LOCAL, max_pages):
-                index = jnp.clip(table_ref[r, k] - spill_base, 0, spill_slots - 1)
-                pages.append(jnp.where(far, far_ref[index], spill_ref[index]))
+            pages = [
+                spill_ref[jnp.clip(table_ref[r, k] - spill_base, 0, spill_slots - 1)]
+                for k in range(LOCAL, max_pages)
+            ]
             ml = ml_ref[r]
             state = (ml[:, 0:1], ml[:, 1:2], a_ref[r])
             _, total, accum = merge([state] + page_blocks(q_all, pages, LOCAL, length))
@@ -170,7 +166,7 @@
     own_slots = requests * LOCAL
     ring = lax.axis_size("req")
     spill_source = pool_slots[own_slots:]
-    spill = lax.ppermute(spill_source, "req", [(i + 1, i) for i in range(ring - 1)])
+    spill = lax.ppermute(spill_source, "req", [((i + 1) % ring, i) for i in range(ring)])
     tree_rows = tree_kv[:, 0, :]
     smem = pl.BlockSpec(memory_space=pltpu.SMEM)
     vmem = pl.BlockSpec(memory_space=pltpu.VMEM)
@@ -188,15 +184,12 @@
     kept, packed, accum = local_call(
         page_table, cache_len, accepted, parents, queries, tree_rows, pool_slots
     )
-    kept, packed, accum, spill_source = lax.optimization_barrier((kept, packed, accum, spill_source))
-    far_spill = lax.ppermute(spill_source, "req", [(0, ring - 1)])
-    far_flag = (lax.axis_index("req") == ring - 1).astype(jnp.int32).reshape(1)
     attention = pl.pallas_call(
         functools.partial(spill_kernel, own_slots),
         out_shape=jax.ShapeDtypeStruct(queries.shape, jnp.bfloat16),
-        in_specs=[smem, smem, smem, vmem, vmem, vmem, vmem, vmem],
+        in_specs=[smem, smem, vmem, vmem, vmem, vmem],
         out_specs=vmem,
-    )(page_table, cache_len, far_flag, packed, accum, queries, spill, far_spill)
+    )(page_table, cache_len, packed, accum, queries, spill)
 
     partial = jnp.dot(attention, o_weight, preferred_element_type=jnp.float32)
     parts = lax.axis_size("tp")

time: 46.5 us -> 41.7 us (0.90)
  waiting for transfers between devices: 4.92 us -> 2.38 us
  starting transfers between devices: 15.1 us -> 13 us
    ppermute x2 -> x1, waiting for transfers between devices: 4.92 us -> 2.38 us  [step(): lax.ppermute(spill_source, 'req', [((i + 1) % ring, i) for i in range(rin...]
    ppermute x2 -> x1, starting transfers between devices: 15.1 us -> 13 us  [step(): lax.ppermute(spill_source, 'req', [((i + 1) % ring, i) for i in range(rin...]
  transfers between devices with their start and end apart: 2 -> 1, of which waited for: 1 -> 1; matrix products, arithmetic and copies ran while one was open for 0% -> 0% of each run, Pallas kernels for 0% -> 11%
where the time goes in v6:
time: 41.7 us; the launch traced here: 41.5 us
  starting transfers between devices  13 us (31%)
  blocking collectives  11 us (26%)
  Pallas kernels  10.1 us (24%)
  waiting for transfers between devices  2.38 us (6%)
  local copies, waits for them, and re-layouts  2.03 us (5%)
  matrix products  1.58 us (4%)
  other arithmetic  0.7 us (2%)
  between operations  0.66 us (2%)
    ppermute x1, starting transfers between devices, step(): lax.ppermute(spill_source, 'req', [((i + 1) % ring, i) for i in range(rin...  13 us
    all_to_all x1, blocking collectives, step(): lax.all_to_all(partial.astype(jnp.bfloat16), 'tp', 0, 0, tiled=True)  11 us
    pallas_call x1, Pallas kernels, step(): pl.pallas_call(functools.partial(spill_kernel, own_slots), out_shape=jax....  5.53 us
    pallas_call x1, Pallas kernels, step(): local_call(page_table, cache_len, accepted, parents, queries, tree_rows,...  4.62 us
    ppermute x1, waiting for transfers between devices, step(): lax.ppermute(spill_source, 'req', [((i + 1) % ring, i) for i in range(rin...  2.38 us
    slice x1, local copies, waits for them, and re-layouts, step(): spill_source = pool_slots[own_slots:]  2.02 us
    dot_general x1, matrix products, step(): partial = jnp.dot(attention, o_weight, preferred_element_type=jnp.float32)  1.58 us
  transfers between devices with their start and end apart: 1, of which 1 were waited for; matrix products, arithmetic and copies ran while one was open for 0% of the time, Pallas kernels for 11%

profile of v6, /device:TPU:8, one launch (start us, length us, event | category | flops | bytes accessed | tf_op | source)
XLA Modules:
  0.0 41.5 jit_solution(15617014554852720552)
XLA Ops:
  0.6 0.0 copy-start
  0.6 2.0 %slice_bitcast_fusion = bf16[8,128,256]{2,1,0:T(8,128)(2,1)} fusion(bf16[12,1,128,256]{3,2,0,1:T(8,128)(2,1)} %bitcast.11), kind=kLoop, calls=%fused_computation.1 | loop fusion | bytes 1048576 | tf_op jit(solution)/shard_map/slice | solution.py:168
  2.7 13.0 %collective-permute-start = (bf16[8,128,256]{2,1,0:T(8,128)(2,1)}, bf16[8,128,256]{2,1,0:T(8,128)(2,1)}, u32[]{:S(2)}, u32[]{:S(2)}) collective-permute-start(bf16[8,128,256]{2,1,0:T(8,128)(2,1)} %slice_bitcast_fusion), channel_id=1, source_target_pairs={{4,0},{8,4},{12,8},{16,12},{20,16},{24,20},{28,24},{32,28},{36,32}... | collective-permute-start | bytes 1572872 | tf_op jit(solution)/shard_map/ppermute | solution.py:169
  15.7 4.6 %shard_map.95 = (bf16[128,256]{1,0:T(8,128)(2,1)}, f32[2,448,128]{2,1,0:T(8,128)}, f32[2,448,128]{2,1,0:T(8,128)}) custom-call(s32[2,8]{1,0:T(2,128)} %table_ref.3, s32[2]{0:T(128)} %len_ref.3, s32[2]{0:T(128)} %leaf_ref.1, s32[2,64]{1,0:T(2,128)} %parents_ref.1, bf16[128,896]{1,0:T(8,128)(2,1)} %q_ref.3, bf16[128,256]{1,0:T(8,128)(2,1)} %bitcast.14, ...), custom_call_target="tpu_custom_call" | custom-call | tf_op jit(solution)/shard_map/pallas_call | solution.py:184
  20.3 2.4 %collective-permute-done.spill_ref = bf16[8,128,256]{2,1,0:T(8,128)(2,1)} collective-permute-done((bf16[8,128,256]{2,1,0:T(8,128)(2,1)}, bf16[8,128,256]{2,1,0:T(8,128)(2,1)}, u32[]{:S(2)}, u32[]{:S(2)}) %collective-permute-start) | collective-permute-done | bytes 524320 | tf_op jit(solution)/shard_map/ppermute | solution.py:169
  22.7 5.5 %shard_map.96 = bf16[128,896]{1,0:T(8,128)(2,1)} custom-call(s32[2,8]{1,0:T(2,128)} %table_ref.3, s32[2]{0:T(128)} %len_ref.3, f32[2,448,128]{2,1,0:T(8,128)} %get-tuple-element.5.ml_ref, f32[2,448,128]{2,1,0:T(8,128)} %get-tuple-element.6.a_ref, bf16[128,896]{1,0:T(8,128)(2,1)} %q_ref.3, bf16[8,128,256]{2,1,0:T(8,128)(2,1)} %collective-permute-done.spill_ref), custom_call_target="tpu_custom_call" | custom-call | tf_op jit(solution)/shard_map/pallas_call | solution.py:187
  28.2 0.0 copy-done
  28.2 1.6 %convolution_convert_fusion = bf16[128,1792]{1,0:T(8,128)(2,1)S(1)} fusion(bf16[128,896]{1,0:T(8,128)(2,1)} %shard_map.96, bf16[896,1792]{1,0:T(8,128)(2,1)S(1)} %copy-done), kind=kOutput, calls=%fused_computation | convolution fusion | flops 411271168 | bytes 3899392 | tf_op jit(solution)/shard_map/dot_general | solution.py:194
  29.8 11.0 %all_to_all.9 = bf16[4,32,1792]{2,1,0:T(8,128)(2,1)S(1)} all-to-all(bf16[4,32,1792]{2,1,0:T(8,128)(2,1)S(1)} %bitcast.13), channel_id=1, replica_groups=mesh['req'=128,'tp'=4] {'tp'}, dimensions={0} | all-to-all | bytes 917504 | tf_op jit(solution)/shard_map/all_to_all | solution.py:196
  40.8 0.7 %fusion = bf16[32,1792]{1,0:T(8,128)(2,1)} fusion(bf16[4,32,1792]{2,1,0:T(8,128)(2,1)S(1)} %all_to_all.9), kind=kLoop, calls=%fused_computation.3 | loop fusion | flops 458752 | bytes 573440 | tf_op jit(solution)/shard_map/add | solution.py:200
Async XLA Ops:
  0.6 27.6 %copy-start = (bf16[896,1792]{1,0:T(8,128)(2,1)S(1)}, bf16[896,1792]{1,0:T(8,128)(2,1)}, u32[]{:S(2)}) copy-start(bf16[896,1792]{1,0:T(8,128)(2,1)} %param.15) | copy-start | bytes 9633796
  2.7 20.0 %collective-permute-start = (bf16[8,128,256]{2,1,0:T(8,128)(2,1)}, bf16[8,128,256]{2,1,0:T(8,128)(2,1)}, u32[]{:S(2)}, u32[]{:S(2)}) collective-permute-start(bf16[8,128,256]{2,1,0:T(8,128)(2,1)} %slice_bitcast_fusion), channel_id=1, source_target_pairs={{4,0},{8,4},{12,8},{16,12},{20,16},{24,20},{28,24},{32,28},{36,32}... | collective-permute-start | bytes 1572872 | tf_op jit(solution)/shard_map/ppermute | solution.py:169

commit v7 on v6

--- a/solution.py
+++ b/solution.py
@@ -57,14 +57,19 @@
     return top, total, accum
 
 
-def local_kernel(
-    table_ref, len_ref, leaf_ref, parents_ref, q_ref, tree_ref, pool_ref,
-    kept_ref, ml_ref, a_ref,
+def merged_kernel(
+    spill_base, table_ref, len_ref, leaf_ref, parents_ref, q_ref, tree_ref, pool_ref, spill_ref,
+    weight_hbm, proj_ref, kept_ref, weight_vmem, att_sc, weight_sem,
 ):
+    weight_copy = pltpu.make_async_copy(weight_hbm, weight_vmem, weight_sem)
+    weight_copy.start()
+
     n_req, tree_len = parents_ref.shape
     nodes = n_req * tree_len
     heads = q_ref.shape[1] // HEAD_SIZE
     stacked = heads * tree_len
+    max_pages = table_ref.shape[1]
+    spill_slots = spill_ref.shape[0]
     scale = 1.0 / math.sqrt(HEAD_SIZE)
     sub = lax.broadcasted_iota(jnp.int32, (nodes, nodes), 0)
     lane = lax.broadcasted_iota(jnp.int32, (nodes, nodes), 1)
@@ -117,51 +122,29 @@
     l = jnp.sum(w.astype(jnp.float32), axis=1, keepdims=True)
     a = jnp.dot(w, tree_rows[:, HEAD_SIZE:], preferred_element_type=jnp.float32)
 
-    state_lane = lax.broadcasted_iota(jnp.int32, (stacked, HEAD_SIZE), 1)
     for r in range(n_req):
         rows = slice(r * stacked, (r + 1) * stacked)
         pages = [pool_ref[table_ref[r, k]] for k in range(LOCAL)]
+        pages += [
+            spill_ref[jnp.clip(table_ref[r, k] - spill_base, 0, spill_slots - 1)]
+            for k in range(LOCAL, max_pages)
+        ]
         blocks = [(m[rows], l[rows], a[rows])] + page_blocks(q_all[r], pages, 0, len_ref[r])
-        top, total, accum = merge(blocks)
-        ml_ref[r] = jnp.where(state_lane == 0, top, jnp.where(state_lane == 1, total, 0.0))
-        a_ref[r] = accum
+        _, total, accum = merge(blocks)
+        att = (accum / total).astype(att_sc.dtype)
+        for g in range(heads):
+            att_sc[pl.ds(r * tree_len, tree_len), pl.ds(g * HEAD_SIZE, HEAD_SIZE)] = att[
+                g * tree_len : (g + 1) * tree_len
+            ]
 
-
-def spill_kernel(spill_base, table_ref, len_ref, ml_ref, a_ref, q_ref, spill_ref, att_ref):
-    n_req, tree_len = table_ref.shape[0], q_ref.shape[0] // table_ref.shape[0]
-    heads = q_ref.shape[1] // HEAD_SIZE
-    max_pages = table_ref.shape[1]
-    spill_slots = spill_ref.shape[0]
-    page_len = spill_ref.shape[1]
-    for r in range(n_req):
-        rows = pl.ds(r * tree_len, tree_len)
-        length = len_ref[r]
-
-        def write(att):
-            for g in range(heads):
-                att_ref[rows, pl.ds(g * HEAD_SIZE, HEAD_SIZE)] = att[g * tree_len : (g + 1) * tree_len]
-
-        @pl.when(length > LOCAL * page_len)
-        def _():
-            q_all = stacked_queries(q_ref, rows, heads)
-            pages = [
-                spill_ref[jnp.clip(table_ref[r, k] - spill_base, 0, spill_slots - 1)]
-                for k in range(LOCAL, max_pages)
-            ]
-            ml = ml_ref[r]
-            state = (ml[:, 0:1], ml[:, 1:2], a_ref[r])
-            _, total, accum = merge([state] + page_blocks(q_all, pages, LOCAL, length))
-            write((accum / total).astype(att_ref.dtype))
-
-        @pl.when(length <= LOCAL * page_len)
-        def _():
-            ml = ml_ref[r]
-            write((a_ref[r] / ml[:, 1:2]).astype(att_ref.dtype))
+    weight_copy.wait()
+    proj_ref[...] = jnp.dot(
+        att_sc[...], weight_vmem[...], preferred_element_type=jnp.float32
+    ).astype(proj_ref.dtype)
 
 
 def step(queries, tree_kv, page_pool, page_table, cache_len, parents, accepted, o_weight):
-    requests, tree_len = parents.shape
-    heads = queries.shape[1] // HEAD_SIZE
+    requests, _ = parents.shape
     pool_slots = page_pool[:, 0]
     own_slots = requests * LOCAL
     ring = lax.axis_size("req")
@@ -170,30 +153,25 @@
     tree_rows = tree_kv[:, 0, :]
     smem = pl.BlockSpec(memory_space=pltpu.SMEM)
     vmem = pl.BlockSpec(memory_space=pltpu.VMEM)
-    stacked = heads * tree_len
-    local_call = pl.pallas_call(
-        local_kernel,
+    merged_call = pl.pallas_call(
+        functools.partial(merged_kernel, own_slots),
         out_shape=(
+            jax.ShapeDtypeStruct((queries.shape[0], o_weight.shape[1]), jnp.bfloat16),
             jax.ShapeDtypeStruct(tree_rows.shape, jnp.bfloat16),
-            jax.ShapeDtypeStruct((requests, stacked, HEAD_SIZE), jnp.float32),
-            jax.ShapeDtypeStruct((requests, stacked, HEAD_SIZE), jnp.float32),
         ),
-        in_specs=[smem, smem, smem, vmem, vmem, vmem, vmem],
-        out_specs=(vmem, vmem, vmem),
+        in_specs=[smem, smem, smem, vmem, vmem, vmem, vmem, vmem, pl.BlockSpec(memory_space=pl.ANY)],
+        out_specs=(vmem, vmem),
+        scratch_shapes=[
+            pltpu.VMEM(o_weight.shape, o_weight.dtype),
+            pltpu.VMEM(queries.shape, jnp.bfloat16),
+            pltpu.SemaphoreType.DMA(()),
+        ],
     )
-    kept, packed, accum = local_call(
-        page_table, cache_len, accepted, parents, queries, tree_rows, pool_slots
+    partial, kept = merged_call(
+        page_table, cache_len, accepted, parents, queries, tree_rows, pool_slots, spill, o_weight
     )
-    attention = pl.pallas_call(
-        functools.partial(spill_kernel, own_slots),
-        out_shape=jax.ShapeDtypeStruct(queries.shape, jnp.bfloat16),
-        in_specs=[smem, smem, vmem, vmem, vmem, vmem],
-        out_specs=vmem,
-    )(page_table, cache_len, packed, accum, queries, spill)
-
-    partial = jnp.dot(attention, o_weight, preferred_element_type=jnp.float32)
     parts = lax.axis_size("tp")
-    gathered = lax.all_to_all(partial.astype(jnp.bfloat16), "tp", 0, 0, tiled=True)
+    gathered = lax.all_to_all(partial, "tp", 0, 0, tiled=True)
     blocks = gathered.reshape(parts, partial.shape[0] // parts, partial.shape[1])
     summed = blocks[0].astype(jnp.float32)
     for i in range(1, parts):

time: 41.7 us -> 42.3 us (1.014)
  waiting for transfers between devices: 2.38 us -> 6.68 us
  Pallas kernels: 10.1 us -> 7.88 us
  matrix products: 1.58 us -> 0 us
    ppermute x1, waiting for transfers between devices: 2.38 us -> 6.68 us  [step(): lax.ppermute(spill_source, 'req', [((i + 1) % ring, i) for i in range(rin...]
    pallas_call x2 -> x1, Pallas kernels: 10.1 us -> 7.88 us  [step(): merged_call(page_table, cache_len, accepted, parents, queries, tree_rows,...]
    dot_general x1 -> x0, matrix products: 1.58 us -> none  [step(): partial = jnp.dot(attention, o_weight, preferred_element_type=jnp.float32)]
    slice x1, local copies, waits for them, and re-layouts: 2.02 us -> 1.08 us  [step(): spill_source = pool_slots[own_slots:]]
    unnamed x2, local copies, waits for them, and re-layouts: 0.01 us -> 0.79 us
  transfers between devices with their start and end apart: 1 -> 1, of which waited for: 1 -> 1; matrix products, arithmetic and copies ran while one was open for 0% -> 0% of each run, Pallas kernels for 11% -> 0%
where the time goes in v7:
time: 42.3 us; the launch traced here: 42 us
  starting transfers between devices  13 us (31%)
  blocking collectives  11.2 us (26%)
  Pallas kernels  7.88 us (19%)
  waiting for transfers between devices  6.68 us (16%)
  local copies, waits for them, and re-layouts  1.87 us (4%)
  other arithmetic  0.7 us (2%)
  between operations  0.65 us (2%)
    ppermute x1, starting transfers between devices, step(): lax.ppermute(spill_source, 'req', [((i + 1) % ring, i) for i in range(rin...  13 us
    all_to_all x1, blocking collectives, step(): gathered = lax.all_to_all(partial, 'tp', 0, 0, tiled=True)  11.2 us
    pallas_call x1, Pallas kernels, step(): merged_call(page_table, cache_len, accepted, parents, queries, tree_rows,...  7.88 us
    ppermute x1, waiting for transfers between devices, step(): lax.ppermute(spill_source, 'req', [((i + 1) % ring, i) for i in range(rin...  6.68 us
    slice x1, local copies, waits for them, and re-layouts, step(): spill_source = pool_slots[own_slots:]  1.08 us
  transfers between devices with their start and end apart: 1, of which 1 were waited for; matrix products, arithmetic and copies ran while one was open for 0% of the time, Pallas kernels for 0%

profile of v7, /device:TPU:8, one launch (start us, length us, event | category | flops | bytes accessed | tf_op | source)
XLA Modules:
  0.0 42.0 jit_solution(5718988648835119190)
XLA Ops:
  0.6 1.1 %slice_bitcast_fusion = bf16[8,128,256]{2,1,0:T(8,128)(2,1)S(1)} fusion(bf16[12,1,128,256]{3,2,0,1:T(8,128)(2,1)} %bitcast.9), kind=kLoop, calls=%fused_computation | loop fusion | bytes 1048576 | tf_op jit(solution)/shard_map/slice | solution.py:151
  1.7 13.0 %collective-permute-start = (bf16[8,128,256]{2,1,0:T(8,128)(2,1)S(1)}, bf16[8,128,256]{2,1,0:T(8,128)(2,1)S(1)}, u32[]{:S(2)}, u32[]{:S(2)}) collective-permute-start(bf16[8,128,256]{2,1,0:T(8,128)(2,1)S(1)} %slice_bitcast_fusion), channel_id=1, source_target_pairs={{4,0},{8,4},{12,8},{16,12},{20,16},{24,20},{28,24},{32,28},{36,32}... | collective-permute-start | bytes 1572872 | tf_op jit(solution)/shard_map/ppermute | solution.py:152
  14.8 6.7 %collective-permute-done.spill_ref = bf16[8,128,256]{2,1,0:T(8,128)(2,1)S(1)} collective-permute-done((bf16[8,128,256]{2,1,0:T(8,128)(2,1)S(1)}, bf16[8,128,256]{2,1,0:T(8,128)(2,1)S(1)}, u32[]{:S(2)}, u32[]{:S(2)}) %collective-permute-start) | collective-permute-done | bytes 524320 | tf_op jit(solution)/shard_map/ppermute | solution.py:152
  21.4 0.0 copy-start
  21.4 0.8 %copy-done = bf16[8,128,256]{2,1,0:T(8,128)(2,1)} copy-done((bf16[8,128,256]{2,1,0:T(8,128)(2,1)}, bf16[8,128,256]{2,1,0:T(8,128)(2,1)S(1)}, u32[]{:S(2)}) %copy-start) | copy-done | bytes 524312
  22.2 7.9 %shard_map.95 = (bf16[128,1792]{1,0:T(8,128)(2,1)}, bf16[128,256]{1,0:T(8,128)(2,1)}) custom-call(s32[2,8]{1,0:T(2,128)} %table_ref.1, s32[2]{0:T(128)} %len_ref.1, s32[2]{0:T(128)} %leaf_ref.1, s32[2,64]{1,0:T(2,128)} %parents_ref.1, bf16[128,896]{1,0:T(8,128)(2,1)} %q_ref.1, bf16[128,256]{1,0:T(8,128)(2,1)} %bitcast.12, bf16[12,128,256]{2,1,0:T(8,128)(2,1)} %bitcast.10, ...), custom_call_target="tpu_custom_call" | custom-call | tf_op jit(solution)/shard_map/pallas_call | solution.py:170
  30.1 11.2 %all_to_all.9 = bf16[4,32,1792]{2,1,0:T(8,128)(2,1)S(1)} all-to-all(bf16[4,32,1792]{2,1,0:T(8,128)(2,1)} %bitcast.11), channel_id=1, replica_groups=mesh['req'=128,'tp'=4] {'tp'}, dimensions={0} | all-to-all | bytes 917504 | tf_op jit(solution)/shard_map/all_to_all | solution.py:174
  41.3 0.7 %fusion = bf16[32,1792]{1,0:T(8,128)(2,1)} fusion(bf16[4,32,1792]{2,1,0:T(8,128)(2,1)S(1)} %all_to_all.9), kind=kLoop, calls=%fused_computation.2 | loop fusion | flops 458752 | bytes 573440 | tf_op jit(solution)/shard_map/add | solution.py:178
Async XLA Ops:
  1.7 19.7 %collective-permute-start = (bf16[8,128,256]{2,1,0:T(8,128)(2,1)S(1)}, bf16[8,128,256]{2,1,0:T(8,128)(2,1)S(1)}, u32[]{:S(2)}, u32[]{:S(2)}) collective-permute-start(bf16[8,128,256]{2,1,0:T(8,128)(2,1)S(1)} %slice_bitcast_fusion), channel_id=1, source_target_pairs={{4,0},{8,4},{12,8},{16,12},{20,16},{24,20},{28,24},{32,28},{36,32}... | collective-permute-start | bytes 1572872 | tf_op jit(solution)/shard_map/ppermute | solution.py:152
  21.4 0.8 %copy-start = (bf16[8,128,256]{2,1,0:T(8,128)(2,1)}, bf16[8,128,256]{2,1,0:T(8,128)(2,1)S(1)}, u32[]{:S(2)}) copy-start(bf16[8,128,256]{2,1,0:T(8,128)(2,1)S(1)} %collective-permute-done.spill_ref) | copy-start | bytes 1572868

commit v8 on v6

--- a/solution.py
+++ b/solution.py
@@ -127,7 +127,12 @@
         a_ref[r] = accum
 
 
-def spill_kernel(spill_base, table_ref, len_ref, ml_ref, a_ref, q_ref, spill_ref, att_ref):
+def spill_kernel(
+    spill_base, table_ref, len_ref, ml_ref, a_ref, q_ref, spill_ref, weight_hbm,
+    proj_ref, weight_vmem, att_sc, weight_sem,
+):
+    weight_copy = pltpu.make_async_copy(weight_hbm, weight_vmem, weight_sem)
+    weight_copy.start()
     n_req, tree_len = table_ref.shape[0], q_ref.shape[0] // table_ref.shape[0]
     heads = q_ref.shape[1] // HEAD_SIZE
     max_pages = table_ref.shape[1]
@@ -139,7 +144,7 @@
 
         def write(att):
             for g in range(heads):
-                att_ref[rows, pl.ds(g * HEAD_SIZE, HEAD_SIZE)] = att[g * tree_len : (g + 1) * tree_len]
+                att_sc[rows, pl.ds(g * HEAD_SIZE, HEAD_SIZE)] = att[g * tree_len : (g + 1) * tree_len]
 
         @pl.when(length > LOCAL * page_len)
         def _():
@@ -151,12 +156,17 @@
             ml = ml_ref[r]
             state = (ml[:, 0:1], ml[:, 1:2], a_ref[r])
             _, total, accum = merge([state] + page_blocks(q_all, pages, LOCAL, length))
-            write((accum / total).astype(att_ref.dtype))
+            write((accum / total).astype(att_sc.dtype))
 
         @pl.when(length <= LOCAL * page_len)
         def _():
             ml = ml_ref[r]
-            write((a_ref[r] / ml[:, 1:2]).astype(att_ref.dtype))
+            write((a_ref[r] / ml[:, 1:2]).astype(att_sc.dtype))
+
+    weight_copy.wait()
+    proj_ref[...] = jnp.dot(
+        att_sc[...], weight_vmem[...], preferred_element_type=jnp.float32
+    ).astype(proj_ref.dtype)
 
 
 def step(queries, tree_kv, page_pool, page_table, cache_len, parents, accepted, o_weight):
@@ -184,16 +194,20 @@
     kept, packed, accum = local_call(
         page_table, cache_len, accepted, parents, queries, tree_rows, pool_slots
     )
-    attention = pl.pallas_call(
+    partial = pl.pallas_call(
         functools.partial(spill_kernel, own_slots),
-        out_shape=jax.ShapeDtypeStruct(queries.shape, jnp.bfloat16),
-        in_specs=[smem, smem, vmem, vmem, vmem, vmem],
+        out_shape=jax.ShapeDtypeStruct((queries.shape[0], o_weight.shape[1]), jnp.bfloat16),
+        in_specs=[smem, smem, vmem, vmem, vmem, vmem, pl.BlockSpec(memory_space=pl.ANY)],
         out_specs=vmem,
-    )(page_table, cache_len, packed, accum, queries, spill)
-
-    partial = jnp.dot(attention, o_weight, preferred_element_type=jnp.float32)
+        scratch_shapes=[
+            pltpu.VMEM(o_weight.shape, o_weight.dtype),
+            pltpu.VMEM(queries.shape, jnp.bfloat16),
+            pltpu.SemaphoreType.DMA(()),
+        ],
+    )(page_table, cache_len, packed, accum, queries, spill, o_weight)
+
     parts = lax.axis_size("tp")
-    gathered = lax.all_to_all(partial.astype(jnp.bfloat16), "tp", 0, 0, tiled=True)
+    gathered = lax.all_to_all(partial, "tp", 0, 0, tiled=True)
     blocks = gathered.reshape(parts, partial.shape[0] // parts, partial.shape[1])
     summed = blocks[0].astype(jnp.float32)
     for i in range(1, parts):

time: 41.7 us -> 40.7 us (0.976)
  matrix products: 1.58 us -> 0 us
  Pallas kernels: 10.1 us -> 10.8 us
    dot_general x1 -> x0, matrix products: 1.58 us -> none  [step(): partial = jnp.dot(attention, o_weight, preferred_element_type=jnp.float32)]
    slice x1, local copies, waits for them, and re-layouts: 2.02 us -> 1.08 us  [step(): spill_source = pool_slots[own_slots:]]
    unnamed x2, local copies, waits for them, and re-layouts: 0.01 us -> 0.79 us
    pallas_call x1, Pallas kernels: 5.53 us -> 6.27 us  [step(): pl.pallas_call(functools.partial(spill_kernel, own_slots), out_shape=jax....]
where the time goes in v8:
time: 40.7 us; the launch traced here: 40.4 us
  starting transfers between devices  13 us (32%)
  blocking collectives  11.2 us (28%)
  Pallas kernels  10.8 us (27%)
  waiting for transfers between devices  2.1 us (5%)
  local copies, waits for them, and re-layouts  1.87 us (5%)
  other arithmetic  0.7 us (2%)
  between operations  0.65 us (2%)
    ppermute x1, starting transfers between devices, step(): lax.ppermute(spill_source, 'req', [((i + 1) % ring, i) for i in range(rin...  13 us
    all_to_all x1, blocking collectives, step(): gathered = lax.all_to_all(partial, 'tp', 0, 0, tiled=True)  11.2 us
    pallas_call x1, Pallas kernels, step(): pl.pallas_call(functools.partial(spill_kernel, own_slots), out_shape=jax....  6.27 us
    pallas_call x1, Pallas kernels, step(): local_call(page_table, cache_len, accepted, parents, queries, tree_rows,...  4.58 us
    ppermute x1, waiting for transfers between devices, step(): lax.ppermute(spill_source, 'req', [((i + 1) % ring, i) for i in range(rin...  2.1 us
    slice x1, local copies, waits for them, and re-layouts, step(): spill_source = pool_slots[own_slots:]  1.08 us
  transfers between devices with their start and end apart: 1, of which 1 were waited for; matrix products, arithmetic and copies ran while one was open for 0% of the time, Pallas kernels for 11%

profile of v8, /device:TPU:8, one launch (start us, length us, event | category | flops | bytes accessed | tf_op | source)
XLA Modules:
  0.0 40.4 jit_solution(2916120810012417165)
XLA Ops:
  0.6 1.1 %slice_bitcast_fusion = bf16[8,128,256]{2,1,0:T(8,128)(2,1)S(1)} fusion(bf16[12,1,128,256]{3,2,0,1:T(8,128)(2,1)} %bitcast.9), kind=kLoop, calls=%fused_computation | loop fusion | bytes 1048576 | tf_op jit(solution)/shard_map/slice | solution.py:178
  1.7 13.0 %collective-permute-start = (bf16[8,128,256]{2,1,0:T(8,128)(2,1)S(1)}, bf16[8,128,256]{2,1,0:T(8,128)(2,1)S(1)}, u32[]{:S(2)}, u32[]{:S(2)}) collective-permute-start(bf16[8,128,256]{2,1,0:T(8,128)(2,1)S(1)} %slice_bitcast_fusion), channel_id=1, source_target_pairs={{4,0},{8,4},{12,8},{16,12},{20,16},{24,20},{28,24},{32,28},{36,32}... | collective-permute-start | bytes 1572872 | tf_op jit(solution)/shard_map/ppermute | solution.py:179
  14.8 4.6 %shard_map.95 = (bf16[128,256]{1,0:T(8,128)(2,1)}, f32[2,448,128]{2,1,0:T(8,128)}, f32[2,448,128]{2,1,0:T(8,128)}) custom-call(s32[2,8]{1,0:T(2,128)} %table_ref.3, s32[2]{0:T(128)} %len_ref.3, s32[2]{0:T(128)} %leaf_ref.1, s32[2,64]{1,0:T(2,128)} %parents_ref.1, bf16[128,896]{1,0:T(8,128)(2,1)} %q_ref.3, bf16[128,256]{1,0:T(8,128)(2,1)} %bitcast.12, ...), custom_call_target="tpu_custom_call" | custom-call | tf_op jit(solution)/shard_map/pallas_call | solution.py:194
  19.3 2.1 %collective-permute-done.spill_ref = bf16[8,128,256]{2,1,0:T(8,128)(2,1)S(1)} collective-permute-done((bf16[8,128,256]{2,1,0:T(8,128)(2,1)S(1)}, bf16[8,128,256]{2,1,0:T(8,128)(2,1)S(1)}, u32[]{:S(2)}, u32[]{:S(2)}) %collective-permute-start) | collective-permute-done | bytes 524320 | tf_op jit(solution)/shard_map/ppermute | solution.py:179
  21.4 0.0 copy-start
  21.4 0.8 %copy-done = bf16[8,128,256]{2,1,0:T(8,128)(2,1)} copy-done((bf16[8,128,256]{2,1,0:T(8,128)(2,1)}, bf16[8,128,256]{2,1,0:T(8,128)(2,1)S(1)}, u32[]{:S(2)}) %copy-start) | copy-done | bytes 524312
  22.2 6.3 %shard_map.96 = bf16[128,1792]{1,0:T(8,128)(2,1)} custom-call(s32[2,8]{1,0:T(2,128)} %table_ref.3, s32[2]{0:T(128)} %len_ref.3, f32[2,448,128]{2,1,0:T(8,128)} %get-tuple-element.5.ml_ref, f32[2,448,128]{2,1,0:T(8,128)} %get-tuple-element.6.a_ref, bf16[128,896]{1,0:T(8,128)(2,1)} %q_ref.3, bf16[8,128,256]{2,1,0:T(8,128)(2,1)} %copy-done, ...), custom_call_target="tpu_custom_call" | custom-call | tf_op jit(solution)/shard_map/pallas_call | solution.py:197
  28.5 11.2 %all_to_all.9 = bf16[4,32,1792]{2,1,0:T(8,128)(2,1)S(1)} all-to-all(bf16[4,32,1792]{2,1,0:T(8,128)(2,1)} %bitcast.11), channel_id=1, replica_groups=mesh['req'=128,'tp'=4] {'tp'}, dimensions={0} | all-to-all | bytes 917504 | tf_op jit(solution)/shard_map/all_to_all | solution.py:210
  39.7 0.7 %fusion = bf16[32,1792]{1,0:T(8,128)(2,1)} fusion(bf16[4,32,1792]{2,1,0:T(8,128)(2,1)S(1)} %all_to_all.9), kind=kLoop, calls=%fused_computation.2 | loop fusion | flops 458752 | bytes 573440 | tf_op jit(solution)/shard_map/add | solution.py:214
Async XLA Ops:
  1.7 19.7 %collective-permute-start = (bf16[8,128,256]{2,1,0:T(8,128)(2,1)S(1)}, bf16[8,128,256]{2,1,0:T(8,128)(2,1)S(1)}, u32[]{:S(2)}, u32[]{:S(2)}) collective-permute-start(bf16[8,128,256]{2,1,0:T(8,128)(2,1)S(1)} %slice_bitcast_fusion), channel_id=1, source_target_pairs={{4,0},{8,4},{12,8},{16,12},{20,16},{24,20},{28,24},{32,28},{36,32}... | collective-permute-start | bytes 1572872 | tf_op jit(solution)/shard_map/ppermute | solution.py:179
  21.4 0.8 %copy-start = (bf16[8,128,256]{2,1,0:T(8,128)(2,1)}, bf16[8,128,256]{2,1,0:T(8,128)(2,1)S(1)}, u32[]{:S(2)}) copy-start(bf16[8,128,256]{2,1,0:T(8,128)(2,1)S(1)} %collective-permute-done.spill_ref) | copy-start | bytes 1572868

commit v9 on v8

--- a/solution.py
+++ b/solution.py
@@ -137,31 +137,19 @@
     heads = q_ref.shape[1] // HEAD_SIZE
     max_pages = table_ref.shape[1]
     spill_slots = spill_ref.shape[0]
-    page_len = spill_ref.shape[1]
     for r in range(n_req):
         rows = pl.ds(r * tree_len, tree_len)
-        length = len_ref[r]
-
-        def write(att):
-            for g in range(heads):
-                att_sc[rows, pl.ds(g * HEAD_SIZE, HEAD_SIZE)] = att[g * tree_len : (g + 1) * tree_len]
-
-        @pl.when(length > LOCAL * page_len)
-        def _():
-            q_all = stacked_queries(q_ref, rows, heads)
-            pages = [
-                spill_ref[jnp.clip(table_ref[r, k] - spill_base, 0, spill_slots - 1)]
-                for k in range(LOCAL, max_pages)
-            ]
-            ml = ml_ref[r]
-            state = (ml[:, 0:1], ml[:, 1:2], a_ref[r])
-            _, total, accum = merge([state] + page_blocks(q_all, pages, LOCAL, length))
-            write((accum / total).astype(att_sc.dtype))
-
-        @pl.when(length <= LOCAL * page_len)
-        def _():
-            ml = ml_ref[r]
-            write((a_ref[r] / ml[:, 1:2]).astype(att_sc.dtype))
+        q_all = stacked_queries(q_ref, rows, heads)
+        pages = [
+            spill_ref[jnp.clip(table_ref[r, k] - spill_base, 0, spill_slots - 1)]
+            for k in range(LOCAL, max_pages)
+        ]
+        ml = ml_ref[r]
+        state = (ml[:, 0:1], ml[:, 1:2], a_ref[r])
+        _, total, accum = merge([state] + page_blocks(q_all, pages, LOCAL, len_ref[r]))
+        att = (accum / total).astype(att_sc.dtype)
+        for g in range(heads):
+            att_sc[rows, pl.ds(g * HEAD_SIZE, HEAD_SIZE)] = att[g * tree_len : (g + 1) * tree_len]
 
     weight_copy.wait()
     proj_ref[...] = jnp.dot(

time: 40.7 us -> 40.7 us (level)
  no operation moved by 1% of the time
where the time goes in v9:
time: 40.7 us; the launch traced here: 40.4 us
  starting transfers between devices  13 us (32%)
  blocking collectives  11.2 us (28%)
  Pallas kernels  10.8 us (27%)
  waiting for transfers between devices  2.1 us (5%)
  local copies, waits for them, and re-layouts  1.87 us (5%)
  other arithmetic  0.7 us (2%)
  between operations  0.65 us (2%)
    ppermute x1, starting transfers between devices, step(): lax.ppermute(spill_source, 'req', [((i + 1) % ring, i) for i in range(rin...  13 us
    all_to_all x1, blocking collectives, step(): gathered = lax.all_to_all(partial, 'tp', 0, 0, tiled=True)  11.2 us
    pallas_call x1, Pallas kernels, step(): pl.pallas_call(functools.partial(spill_kernel, own_slots), out_shape=jax....  6.25 us
    pallas_call x1, Pallas kernels, step(): local_call(page_table, cache_len, accepted, parents, queries, tree_rows,...  4.58 us
    ppermute x1, waiting for transfers between devices, step(): lax.ppermute(spill_source, 'req', [((i + 1) % ring, i) for i in range(rin...  2.1 us
    slice x1, local copies, waits for them, and re-layouts, step(): spill_source = pool_slots[own_slots:]  1.08 us
  transfers between devices with their start and end apart: 1, of which 1 were waited for; matrix products, arithmetic and copies ran while one was open for 0% of the time, Pallas kernels for 11%

profile of v9, /device:TPU:8, one launch (start us, length us, event | category | flops | bytes accessed | tf_op | source)
XLA Modules:
  0.0 40.4 jit_solution(6999635578665560582)
XLA Ops:
  0.6 1.1 %slice_bitcast_fusion = bf16[8,128,256]{2,1,0:T(8,128)(2,1)S(1)} fusion(bf16[12,1,128,256]{3,2,0,1:T(8,128)(2,1)} %bitcast.9), kind=kLoop, calls=%fused_computation | loop fusion | bytes 1048576 | tf_op jit(solution)/shard_map/slice | solution.py:166
  1.7 13.0 %collective-permute-start = (bf16[8,128,256]{2,1,0:T(8,128)(2,1)S(1)}, bf16[8,128,256]{2,1,0:T(8,128)(2,1)S(1)}, u32[]{:S(2)}, u32[]{:S(2)}) collective-permute-start(bf16[8,128,256]{2,1,0:T(8,128)(2,1)S(1)} %slice_bitcast_fusion), channel_id=1, source_target_pairs={{4,0},{8,4},{12,8},{16,12},{20,16},{24,20},{28,24},{32,28},{36,32}... | collective-permute-start | bytes 1572872 | tf_op jit(solution)/shard_map/ppermute | solution.py:167
  14.8 4.6 %shard_map.95 = (bf16[128,256]{1,0:T(8,128)(2,1)}, f32[2,448,128]{2,1,0:T(8,128)}, f32[2,448,128]{2,1,0:T(8,128)}) custom-call(s32[2,8]{1,0:T(2,128)} %table_ref.3, s32[2]{0:T(128)} %len_ref.3, s32[2]{0:T(128)} %leaf_ref.1, s32[2,64]{1,0:T(2,128)} %parents_ref.1, bf16[128,896]{1,0:T(8,128)(2,1)} %q_ref.3, bf16[128,256]{1,0:T(8,128)(2,1)} %bitcast.12, ...), custom_call_target="tpu_custom_call" | custom-call | tf_op jit(solution)/shard_map/pallas_call | solution.py:182
  19.3 2.1 %collective-permute-done.spill_ref = bf16[8,128,256]{2,1,0:T(8,128)(2,1)S(1)} collective-permute-done((bf16[8,128,256]{2,1,0:T(8,128)(2,1)S(1)}, bf16[8,128,256]{2,1,0:T(8,128)(2,1)S(1)}, u32[]{:S(2)}, u32[]{:S(2)}) %collective-permute-start) | collective-permute-done | bytes 524320 | tf_op jit(solution)/shard_map/ppermute | solution.py:167
  21.4 0.0 copy-start
  21.4 0.8 %copy-done = bf16[8,128,256]{2,1,0:T(8,128)(2,1)} copy-done((bf16[8,128,256]{2,1,0:T(8,128)(2,1)}, bf16[8,128,256]{2,1,0:T(8,128)(2,1)S(1)}, u32[]{:S(2)}) %copy-start) | copy-done | bytes 524312
  22.2 6.2 %shard_map.96 = bf16[128,1792]{1,0:T(8,128)(2,1)} custom-call(s32[2,8]{1,0:T(2,128)} %table_ref.3, s32[2]{0:T(128)} %len_ref.3, f32[2,448,128]{2,1,0:T(8,128)} %get-tuple-element.5.ml_ref, f32[2,448,128]{2,1,0:T(8,128)} %get-tuple-element.6.a_ref, bf16[128,896]{1,0:T(8,128)(2,1)} %q_ref.3, bf16[8,128,256]{2,1,0:T(8,128)(2,1)} %copy-done, ...), custom_call_target="tpu_custom_call" | custom-call | tf_op jit(solution)/shard_map/pallas_call | solution.py:185
  28.5 11.2 %all_to_all.9 = bf16[4,32,1792]{2,1,0:T(8,128)(2,1)S(1)} all-to-all(bf16[4,32,1792]{2,1,0:T(8,128)(2,1)} %bitcast.11), channel_id=1, replica_groups=mesh['req'=128,'tp'=4] {'tp'}, dimensions={0} | all-to-all | bytes 917504 | tf_op jit(solution)/shard_map/all_to_all | solution.py:198
  39.7 0.7 %fusion = bf16[32,1792]{1,0:T(8,128)(2,1)} fusion(bf16[4,32,1792]{2,1,0:T(8,128)(2,1)S(1)} %all_to_all.9), kind=kLoop, calls=%fused_computation.2 | loop fusion | flops 458752 | bytes 573440 | tf_op jit(solution)/shard_map/add | solution.py:202
Async XLA Ops:
  1.7 19.7 %collective-permute-start = (bf16[8,128,256]{2,1,0:T(8,128)(2,1)S(1)}, bf16[8,128,256]{2,1,0:T(8,128)(2,1)S(1)}, u32[]{:S(2)}, u32[]{:S(2)}) collective-permute-start(bf16[8,128,256]{2,1,0:T(8,128)(2,1)S(1)} %slice_bitcast_fusion), channel_id=1, source_target_pairs={{4,0},{8,4},{12,8},{16,12},{20,16},{24,20},{28,24},{32,28},{36,32}... | collective-permute-start | bytes 1572872 | tf_op jit(solution)/shard_map/ppermute | solution.py:167
  21.4 0.8 %copy-start = (bf16[8,128,256]{2,1,0:T(8,128)(2,1)}, bf16[8,128,256]{2,1,0:T(8,128)(2,1)S(1)}, u32[]{:S(2)}) copy-start(bf16[8,128,256]{2,1,0:T(8,128)(2,1)S(1)} %collective-permute-done.spill_ref) | copy-start | bytes 1572868

commit v10 on v9

--- a/solution.py
+++ b/solution.py
@@ -157,13 +157,28 @@
     ).astype(proj_ref.dtype)
 
 
+def slot_copy_kernel(first, pool_hbm, out_hbm, sem):
+    copy = pltpu.make_async_copy(pool_hbm.at[pl.ds(first, out_hbm.shape[0])], out_hbm, sem)
+    copy.start()
+    copy.wait()
+
+
 def step(queries, tree_kv, page_pool, page_table, cache_len, parents, accepted, o_weight):
     requests, tree_len = parents.shape
     heads = queries.shape[1] // HEAD_SIZE
     pool_slots = page_pool[:, 0]
     own_slots = requests * LOCAL
     ring = lax.axis_size("req")
-    spill_source = pool_slots[own_slots:]
+    any_space = pl.BlockSpec(memory_space=pl.ANY)
+    spill_source = pl.pallas_call(
+        functools.partial(slot_copy_kernel, own_slots),
+        out_shape=jax.ShapeDtypeStruct(
+            (pool_slots.shape[0] - own_slots,) + pool_slots.shape[1:], pool_slots.dtype
+        ),
+        in_specs=[any_space],
+        out_specs=any_space,
+        scratch_shapes=[pltpu.SemaphoreType.DMA(())],
+    )(pool_slots)
     spill = lax.ppermute(spill_source, "req", [((i + 1) % ring, i) for i in range(ring)])
     tree_rows = tree_kv[:, 0, :]
     smem = pl.BlockSpec(memory_space=pltpu.SMEM)

time: 40.7 us -> 56.9 us (1.40)
  Pallas kernels: 10.8 us -> 27.8 us
  local copies, waits for them, and re-layouts: 1.87 us -> 0.79 us
    pallas_call x0 -> x1, Pallas kernels: none -> 17 us  [step(): pl.pallas_call(functools.partial(slot_copy_kernel, own_slots), out_shape=...]
    slice x1 -> x0, local copies, waits for them, and re-layouts: 1.08 us -> none  [step(): spill_source = pool_slots[own_slots:]]
  transfers between devices with their start and end apart: 1 -> 1, of which waited for: 1 -> 1; matrix products, arithmetic and copies ran while one was open for 0% -> 0% of each run, Pallas kernels for 11% -> 8%
where the time goes in v10:
time: 56.9 us; the launch traced here: 56.6 us
  Pallas kernels  27.8 us (49%)
  starting transfers between devices  13 us (23%)
  blocking collectives  11.2 us (20%)
  waiting for transfers between devices  2.42 us (4%)
  local copies, waits for them, and re-layouts  0.79 us (1%)
  other arithmetic  0.7 us (1%)
  between operations  0.66 us (1%)
    pallas_call x1, Pallas kernels, step(): pl.pallas_call(functools.partial(slot_copy_kernel, own_slots), out_shape=...  17 us
    ppermute x1, starting transfers between devices, step(): lax.ppermute(spill_source, 'req', [((i + 1) % ring, i) for i in range(rin...  13 us
    all_to_all x1, blocking collectives, step(): gathered = lax.all_to_all(partial, 'tp', 0, 0, tiled=True)  11.2 us
    pallas_call x1, Pallas kernels, step(): pl.pallas_call(functools.partial(spill_kernel, own_slots), out_shape=jax....  6.25 us
    pallas_call x1, Pallas kernels, step(): local_call(page_table, cache_len, accepted, parents, queries, tree_rows,...  4.58 us
    ppermute x1, waiting for transfers between devices, step(): lax.ppermute(spill_source, 'req', [((i + 1) % ring, i) for i in range(rin...  2.42 us
  transfers between devices with their start and end apart: 1, of which 1 were waited for; matrix products, arithmetic and copies ran while one was open for 0% of the time, Pallas kernels for 8%

profile of v10, /device:TPU:8, one launch (start us, length us, event | category | flops | bytes accessed | tf_op | source)
XLA Modules:
  0.0 56.6 jit_solution(15295029408689714236)
XLA Ops:
  0.6 17.0 %shard_map.96 = bf16[8,128,256]{2,1,0:T(8,128)(2,1)} custom-call(bf16[12,128,256]{2,1,0:T(8,128)(2,1)} %bitcast.6), custom_call_target="tpu_custom_call" | custom-call | tf_op jit(solution)/shard_map/pallas_call | solution.py:173
  17.6 13.0 %collective-permute-start = (bf16[8,128,256]{2,1,0:T(8,128)(2,1)}, bf16[8,128,256]{2,1,0:T(8,128)(2,1)S(1)}, u32[]{:S(2)}, u32[]{:S(2)}) collective-permute-start(bf16[8,128,256]{2,1,0:T(8,128)(2,1)} %shard_map.96), channel_id=1, source_target_pairs={{4,0},{8,4},{12,8},{16,12},{20,16},{24,20},{28,24},{32,28},{36,32}... | collective-permute-start | bytes 1572872 | tf_op jit(solution)/shard_map/ppermute | solution.py:182
  30.7 4.6 %shard_map.95 = (bf16[128,256]{1,0:T(8,128)(2,1)}, f32[2,448,128]{2,1,0:T(8,128)}, f32[2,448,128]{2,1,0:T(8,128)}) custom-call(s32[2,8]{1,0:T(2,128)} %table_ref.3, s32[2]{0:T(128)} %len_ref.3, s32[2]{0:T(128)} %leaf_ref.1, s32[2,64]{1,0:T(2,128)} %parents_ref.1, bf16[128,896]{1,0:T(8,128)(2,1)} %q_ref.3, bf16[128,256]{1,0:T(8,128)(2,1)} %bitcast.9, ...), custom_call_target="tpu_custom_call" | custom-call | tf_op jit(solution)/shard_map/pallas_call | solution.py:197
  35.3 2.4 %collective-permute-done.spill_ref = bf16[8,128,256]{2,1,0:T(8,128)(2,1)S(1)} collective-permute-done((bf16[8,128,256]{2,1,0:T(8,128)(2,1)}, bf16[8,128,256]{2,1,0:T(8,128)(2,1)S(1)}, u32[]{:S(2)}, u32[]{:S(2)}) %collective-permute-start) | collective-permute-done | bytes 524320 | tf_op jit(solution)/shard_map/ppermute | solution.py:182
  37.7 0.0 copy-start
  37.7 0.8 %copy-done = bf16[8,128,256]{2,1,0:T(8,128)(2,1)} copy-done((bf16[8,128,256]{2,1,0:T(8,128)(2,1)}, bf16[8,128,256]{2,1,0:T(8,128)(2,1)S(1)}, u32[]{:S(2)}) %copy-start) | copy-done | bytes 524312
  38.5 6.2 %shard_map.97 = bf16[128,1792]{1,0:T(8,128)(2,1)} custom-call(s32[2,8]{1,0:T(2,128)} %table_ref.3, s32[2]{0:T(128)} %len_ref.3, f32[2,448,128]{2,1,0:T(8,128)} %get-tuple-element.5.ml_ref, f32[2,448,128]{2,1,0:T(8,128)} %get-tuple-element.6.a_ref, bf16[128,896]{1,0:T(8,128)(2,1)} %q_ref.3, bf16[8,128,256]{2,1,0:T(8,128)(2,1)} %copy-done, ...), custom_call_target="tpu_custom_call" | custom-call | tf_op jit(solution)/shard_map/pallas_call | solution.py:200
  44.7 11.2 %all_to_all.9 = bf16[4,32,1792]{2,1,0:T(8,128)(2,1)S(1)} all-to-all(bf16[4,32,1792]{2,1,0:T(8,128)(2,1)} %bitcast.8), channel_id=1, replica_groups=mesh['req'=128,'tp'=4] {'tp'}, dimensions={0} | all-to-all | bytes 917504 | tf_op jit(solution)/shard_map/all_to_all | solution.py:213
  55.9 0.7 %fusion = bf16[32,1792]{1,0:T(8,128)(2,1)} fusion(bf16[4,32,1792]{2,1,0:T(8,128)(2,1)S(1)} %all_to_all.9), kind=kLoop, calls=%fused_computation.1 | loop fusion | flops 458752 | bytes 573440 | tf_op jit(solution)/shard_map/add | solution.py:217
Async XLA Ops:
  17.6 20.0 %collective-permute-start = (bf16[8,128,256]{2,1,0:T(8,128)(2,1)}, bf16[8,128,256]{2,1,0:T(8,128)(2,1)S(1)}, u32[]{:S(2)}, u32[]{:S(2)}) collective-permute-start(bf16[8,128,256]{2,1,0:T(8,128)(2,1)} %shard_map.96), channel_id=1, source_target_pairs={{4,0},{8,4},{12,8},{16,12},{20,16},{24,20},{28,24},{32,28},{36,32}... | collective-permute-start | bytes 1572872 | tf_op jit(solution)/shard_map/ppermute | solution.py:182
  37.7 0.8 %copy-start = (bf16[8,128,256]{2,1,0:T(8,128)(2,1)}, bf16[8,128,256]{2,1,0:T(8,128)(2,1)S(1)}, u32[]{:S(2)}) copy-start(bf16[8,128,256]{2,1,0:T(8,128)(2,1)S(1)} %collective-permute-done.spill_ref) | copy-start | bytes 1572868
